TPU v7x, 32 devices: a whole 2x2x4 slice. The times are simulated.
32 devices in a mesh: pix: 16 (over z, y, x), mode: 2 (over core).
Axes of the slice: x: 2, y: 2, z: 4, core: 2. Of those that a mesh axis runs over, the one named last changes fastest.
Arguments:
- frames: float32 [384, 49152], P('mode', 'pix'), may hold values from -40 to 40
- basis: float32 [2048, 49152], P('mode', 'pix'), may hold values from -0.078125 to 0.078125
- annulus: int32 [64], P('pix'), may hold values from 0 to 7, as said below
- truncation: int32 [8], replicated, may hold values from 256 to 2048
Outputs:
- residual: float32 [384, 49152], P('mode', 'pix')
Inputs may be any that keep to these rules, and one draw needn't show every extreme that they name: Every annulus holds one block or more; the blocks of an annulus may lie anywhere in the image.
All inputs are finite; a program needn't handle non-finite values.
Results may differ from a plain program's by a relative error of at most 0.0001.
Values sent between devices are 32-bit elements; how exact they have to be, the bound alone decides.
No kernel may reach another device: no remote copies, remote signals or barrier semaphores. Data moves between devices by JAX's collectives and lax.ppermute only.
A program may use at most 128 MiB of HBM per device.

v0:
```python
import jax
import jax.numpy as jnp
from jax import lax
from jax.sharding import PartitionSpec as P

NA = 8
K_CHUNKS = 2


HIGHEST_PRECISION = lax.Precision.HIGHEST


def butterfly_sum(value, axes, size):
    step = 1
    while step < size:
        pairs = [(i, i ^ step) for i in range(size)]
        value = value + lax.ppermute(value, axes, pairs)
        step *= 2
    return value


def local(frames, basis, annulus, truncation):
    own_rows, pix_dev = frames.shape
    groups = lax.axis_size("mode")
    parts = lax.axis_size("pix")
    total_frames = own_rows * groups
    blocks = annulus.shape[0]
    block_len = pix_dev // blocks
    modes_dev = basis.shape[0]
    gathered = lax.all_gather(frames, "mode", axis=0, tiled=True)
    mode_index = lax.axis_index("mode")
    onehot = (annulus[:, None] == jnp.arange(NA, dtype=jnp.int32)[None, :]).astype(jnp.float32)
    own_block_sums = jnp.stack(
        [jnp.sum(frames[:, b * block_len : (b + 1) * block_len], axis=1) for b in range(blocks)],
        axis=0,
    )
    own_sums = jnp.einsum("ba,bf->af", onehot, own_block_sums, precision=HIGHEST_PRECISION)
    frame_slot = (
        mode_index * own_rows + jnp.arange(own_rows, dtype=jnp.int32)
    )[:, None] == jnp.arange(total_frames, dtype=jnp.int32)[None, :]
    local_sums = jnp.einsum(
        "af,fg->ag", own_sums, frame_slot.astype(jnp.float32), precision=HIGHEST_PRECISION
    )
    first_group = (mode_index == 0).astype(jnp.float32)
    local_counts = jnp.sum(onehot, axis=0) * (block_len * first_group)
    own_slot = (
        lax.axis_index("pix") * blocks + jnp.arange(blocks, dtype=jnp.int32)
    )[:, None] == jnp.arange(parts * blocks, dtype=jnp.int32)[None, :]
    local_table = jnp.einsum(
        "ba,bc->ac", onehot, own_slot.astype(jnp.float32), precision=HIGHEST_PRECISION
    ) * first_group
    packed = butterfly_sum(
        jnp.concatenate([local_sums, local_counts[:, None], local_table], axis=1),
        ("pix", "mode"),
        parts * groups,
    )
    annulus_totals = packed[:, :total_frames]
    pixel_counts = packed[:, total_frames]
    every_onehot = packed[:, total_frames + 1 :].T
    every_annulus = jnp.einsum(
        "ba,a->b", every_onehot, jnp.arange(NA, dtype=jnp.float32), precision=HIGHEST_PRECISION
    ).astype(jnp.int32)
    mode_ids = mode_index * modes_dev + jnp.arange(modes_dev, dtype=jnp.int32)
    retained = (mode_ids[None, :] < truncation[:, None]).astype(jnp.float32)
    annulus_means = annulus_totals / pixel_counts[:, None]
    block_means = jnp.einsum("ba,af->bf", onehot, annulus_means, precision=HIGHEST_PRECISION)
    centered = [
        gathered[:, b * block_len : (b + 1) * block_len] - block_means[b][:, None]
        for b in range(blocks)
    ]
    chunk = modes_dev // K_CHUNKS
    rows_dev = total_frames // parts
    pieces = [
        [
            basis[c * chunk : (c + 1) * chunk, b * block_len : (b + 1) * block_len]
            for b in range(blocks)
        ]
        for c in range(K_CHUNKS)
    ]

    def outbound(c):
        per_block = jnp.stack(
            [
                jnp.dot(centered[b], pieces[c][b].T, precision=HIGHEST_PRECISION)
                for b in range(blocks)
            ],
            axis=0,
        )
        return per_block.reshape(blocks, parts, rows_dev, chunk).transpose(1, 0, 2, 3)

    def inbound(c, arrived):
        slice_coefficients = jnp.einsum(
            "ba,bfk->afk",
            every_onehot,
            arrived.reshape(parts * blocks, rows_dev, chunk),
            precision=HIGHEST_PRECISION,
        )
        slice_truncated = slice_coefficients * retained[:, None, c * chunk : (c + 1) * chunk]
        outgoing = jnp.take(slice_truncated, every_annulus, axis=0)
        return outgoing.reshape(parts, blocks, rows_dev, chunk)

    def model_of(c, returned):
        picked = returned.transpose(1, 0, 2, 3).reshape(blocks, total_frames, chunk)
        return jnp.concatenate(
            [jnp.dot(picked[b], pieces[c][b], precision=HIGHEST_PRECISION) for b in range(blocks)],
            axis=1,
        )

    term = None
    pending = None
    for stage in range(K_CHUNKS + 1):
        sending = []
        if stage < K_CHUNKS:
            sending.append(outbound(stage))
        if pending is not None:
            sending.append(pending)
        received = lax.all_to_all(jnp.stack(sending, axis=1), "pix", 0, 0, tiled=True)
        slot = 0
        next_pending = None
        if stage < K_CHUNKS:
            next_pending = inbound(stage, received[:, 0])
            slot = 1
        if pending is not None:
            part = model_of(stage - 1, received[:, slot])
            term = part if term is None else term + part
        pending = next_pending
    model_rows = lax.psum_scatter(term, "mode", scatter_dimension=0, tiled=True)
    own_means = lax.dynamic_slice_in_dim(block_means, mode_index * own_rows, own_rows, 1)
    own_centered = jnp.concatenate(
        [
            frames[:, b * block_len : (b + 1) * block_len] - own_means[b][:, None]
            for b in range(blocks)
        ],
        axis=1,
    )
    return own_centered - model_rows


def solution(mesh):
    return jax.shard_map(
        local,
        mesh=mesh,
        in_specs=(P("mode", "pix"), P("mode", "pix"), P("pix"), P()),
        out_specs=P("mode", "pix"),
        check_vma=False,
    )
```

profile of v0, /device:TPU:0, one launch (start us, length us, event | category | flops | bytes accessed | tf_op | source)
XLA Modules:
  0.0 405.1 jit_solution(1153323173851403167)
XLA Ops:
  28.0 4.1 %fusion.18 = f32[384,512]{1,0:T(8,128)S(1)} fusion(f32[1024,3072]{1,0:T(8,128)} %param.7, f32[384,3072]{1,0:T(8,128)} %all-gather.2.cloned.1.call-done, f32[384]{0:T(512)S(1)} %get-tuple-element.10), kind=kOutput, calls=%fused_computation.29 | convolution fusion | flops 1812234240 | bytes 3540480 | tf_op jit(solution)/shard_map/dot_general | solution.py:84
  32.0 3.9 fusion.14
  36.0 3.6 fusion.10
  39.6 3.6 fusion.6
  45.2 7.7 %all-to-all-start = ((f32[16,1,4,24,512]{4,3,2,1,0:T(8,128)}), f32[16,1,4,24,512]{4,3,2,1,0:T(8,128)}, u32[]{:S(2)}, u32[]{:S(2)}) async-start(f32[16,1,4,24,512]{4,3,2,1,0:T(8,128)} %maximum_bitcast_fusion.1), calls=%async_computation | async-start | bytes 6291456 | tf_op jit(solution)/shard_map/all_to_all | solution.py:117
  53.2 3.9 fusion.34
  57.2 3.9 fusion.30
  61.1 3.9 fusion.26
  65.0 3.9 fusion.22
  70.9 41.3 %all-to-all-done = f32[16,1,4,24,512]{4,3,2,1,0:T(8,128)} async-done(((f32[16,1,4,24,512]{4,3,2,1,0:T(8,128)}), f32[16,1,4,24,512]{4,3,2,1,0:T(8,128)}, u32[]{:S(2)}, u32[]{:S(2)}) %all-to-all-start) | async-done | bytes 3145760 | tf_op jit(solution)/shard_map/all_to_all | solution.py:117
  112.3 5.1 %fusion.36 = f32[8,24,512]{2,0,1:T(8,128)S(1)} fusion(f32[64,24,512]{2,1,0:T(8,128)} %bitcast.32, f32[8,512]{1,0:T(8,128)S(1)} %get-tuple-element.29, f32[8,449]{1,0:T(8,128)S(1)} %add.67), kind=kOutput, calls=%fused_computation.47 | convolution fusion | flops 75595776 | bytes 3559424 | tf_op jit(solution)/shard_map/ba,bfk->afk/dot_general | solution.py:92
  124.5 152.1 %all_to_all.15 = f32[16,2,4,24,512]{4,3,2,1,0:T(8,128)S(1)} all-to-all(f32[16,2,4,24,512]{4,3,2,1,0:T(8,128)S(1)} %pad_maximum_fusion), channel_id=1, replica_groups=mesh['pix'=16,'mode'=2] {'pix'}, dimensions={0} | all-to-all | bytes 12582912 | tf_op jit(solution)/shard_map/all_to_all | solution.py:117
  285.2 3.9 broadcast_select_fusion
  289.1 4.5 %all-to-all-start.2 = ((f32[16,1,4,24,512]{4,3,2,1,0:T(8,128)}), f32[16,1,4,24,512]{4,3,2,1,0:T(8,128)}, u32[]{:S(2)}, u32[]{:S(2)}) async-start(f32[16,1,4,24,512]{4,3,2,1,0:T(8,128)} %bitcast.94), calls=%async_computation.2 | async-start | bytes 6291456 | tf_op jit(solution)/shard_map/all_to_all | solution.py:117
  299.5 4.5 %fusion.16 = f32[384,768]{1,0:T(8,128)} fusion(f32[384,512]{1,0:T(8,128)S(1)} %bitcast.102, f32[1024,3072]{1,0:T(8,128)} %param.7), kind=kOutput, calls=%fused_computation.27 | convolution fusion | flops 1811939328 | bytes 3538944 | tf_op jit(solution)/shard_map/dot_general | solution.py:105
  304.0 4.5 %fusion.4 = f32[384,768]{1,0:T(8,128)} fusion(f32[384,512]{1,0:T(8,128)S(1)} %bitcast.100, f32[1024,3072]{1,0:T(8,128)} %param.7), kind=kOutput, calls=%fused_computation.15 | convolution fusion | flops 1811939328 | bytes 3538944 | tf_op jit(solution)/shard_map/dot_general | solution.py:105
  308.5 4.5 %fusion.8 = f32[384,768]{1,0:T(8,128)} fusion(f32[384,512]{1,0:T(8,128)S(1)} %bitcast.98, f32[1024,3072]{1,0:T(8,128)} %param.7), kind=kOutput, calls=%fused_computation.19 | convolution fusion | flops 1811939328 | bytes 3538944 | tf_op jit(solution)/shard_map/dot_general | solution.py:105
  313.0 40.6 %all-to-all-done.2 = f32[16,1,4,24,512]{4,3,2,1,0:T(8,128)} async-done(((f32[16,1,4,24,512]{4,3,2,1,0:T(8,128)}), f32[16,1,4,24,512]{4,3,2,1,0:T(8,128)}, u32[]{:S(2)}, u32[]{:S(2)}) %all-to-all-start.2) | async-done | bytes 3145760 | tf_op jit(solution)/shard_map/all_to_all | solution.py:117
  356.2 3.5 fusion.20
  359.8 3.5 fusion.24
  363.4 3.9 fusion.28
  367.3 3.5 fusion.32
  374.6 19.9 %reduce-scatter.2.cloned.1.call-done = f32[192,3072]{1,0:T(8,128)} async-done(((f32[384,3072]{1,0:T(8,128)}), f32[192,3072]{1,0:T(8,128)}) %reduce-scatter.2.cloned.1.call-update) | async-done | bytes 2359312 | tf_op jit(solution)/shard_map/reduce_scatter | solution.py:127
  394.4 3.6 maximum_subtract_fusion
  (71 shorter events, 53.6 us)
Async XLA Ops:
  6.5 1.7 copy-start
  6.5 1.9 copy-start.7
  6.5 21.4 %all-gather.2.cloned.1.call-start = ((), (), s32[]{:S(2)}) async-start(), calls=%async_computation.4 | async-start | bytes 7077888 | tf_op jit(solution)/shard_map/all_gather | solution.py:30
  9.3 1.3 collective-permute-start
  10.7 4.5 %collective-permute-start.1 = (f32[8,449]{1,0:T(8,128)S(1)}, f32[8,449]{1,0:T(8,128)S(1)}, u32[]{:S(2)}, u32[]{:S(2)}) collective-permute-start(f32[8,449]{1,0:T(8,128)S(1)} %fusion.90), channel_id=1, source_target_pairs={{0,2},{1,3},{2,0},{3,1},{4,6},{5,7},{6,4},{7,5},{8,10},{9,11},{10,... | collective-permute-start | bytes 43112 | tf_op jit(solution)/shard_map/ppermute | solution.py:17
  15.2 3.8 collective-permute-start.2
  19.0 3.8 collective-permute-start.3
  22.8 4.8 %collective-permute-start.4 = (f32[8,449]{1,0:T(8,128)S(1)}, f32[8,449]{1,0:T(8,128)S(1)}, u32[]{:S(2)}, u32[]{:S(2)}) collective-permute-start(f32[8,449]{1,0:T(8,128)S(1)} %add.66), channel_id=1, source_target_pairs={{0,16},{1,17},{2,18},{3,19},{4,20},{5,21},{6,22},{7,23},{8,24},{9,... | collective-permute-start | bytes 43112 | tf_op jit(solution)/shard_map/ppermute | solution.py:17
  28.0 8.0 %copy-start.1 = (f32[384,3072]{1,0:T(8,128)S(1)}, f32[384,3072]{1,0:T(8,128)}, u32[]{:S(2)}) copy-start(f32[384,3072]{1,0:T(8,128)} %all-gather.2.cloned.1.call-done) | copy-start | bytes 14155780
  45.2 7.7 %copy-start.6 = (s32[8]{0:T(128)S(1)}, s32[8]{0:T(128)}, u32[]{:S(2)}) copy-start(s32[8]{0:T(128)} %param.9) | copy-start | bytes 100
  45.2 67.1 %all-to-all-start = ((f32[16,1,4,24,512]{4,3,2,1,0:T(8,128)}), f32[16,1,4,24,512]{4,3,2,1,0:T(8,128)}, u32[]{:S(2)}, u32[]{:S(2)}) async-start(f32[16,1,4,24,512]{4,3,2,1,0:T(8,128)} %maximum_bitcast_fusion.1), calls=%async_computation | async-start | bytes 6291456 | tf_op jit(solution)/shard_map/all_to_all | solution.py:117
  120.5 2.8 copy-start.2
  289.1 64.6 %all-to-all-start.2 = ((f32[16,1,4,24,512]{4,3,2,1,0:T(8,128)}), f32[16,1,4,24,512]{4,3,2,1,0:T(8,128)}, u32[]{:S(2)}, u32[]{:S(2)}) async-start(f32[16,1,4,24,512]{4,3,2,1,0:T(8,128)} %bitcast.94), calls=%async_computation.2 | async-start | bytes 6291456 | tf_op jit(solution)/shard_map/all_to_all | solution.py:117
  293.6 100.8 %reduce-scatter.2.cloned.1.call-start = ((), (), s32[]{:S(2)}) async-start(), calls=%async_computation.5 | async-start | bytes 7077888 | tf_op jit(solution)/shard_map/reduce_scatter | solution.py:127
  363.3 7.5 %copy-start.3 = (f32[384,768]{1,0:T(8,128)S(1)}, f32[384,768]{1,0:T(8,128)}, u32[]{:S(2)}) copy-start(f32[384,768]{1,0:T(8,128)} %fusion.16) | copy-start | bytes 3538948
  363.3 7.5 %copy-start.4 = (f32[384,768]{1,0:T(8,128)S(1)}, f32[384,768]{1,0:T(8,128)}, u32[]{:S(2)}) copy-start(f32[384,768]{1,0:T(8,128)} %fusion.4) | copy-start | bytes 3538948
  363.3 7.5 %copy-start.5 = (f32[384,768]{1,0:T(8,128)S(1)}, f32[384,768]{1,0:T(8,128)}, u32[]{:S(2)}) copy-start(f32[384,768]{1,0:T(8,128)} %fusion.8) | copy-start | bytes 3538948
Sparse Core Ops, SparseCore 0:
  8.9 17.1 all-gather.1
  373.4 20.9 reduce-scatter.1
where the time goes:
time: 413 us; the launch traced here: 405 us
  blocking collectives  152 us (37%)
  waiting for transfers between devices  110 us (27%)
  matrix products  72 us (17%)
  starting transfers between devices  22.8 us (6%)
  other arithmetic  19.9 us (5%)
  local copies, waits for them, and re-layouts  14 us (3%)
  between operations  13.9 us (3%)
    all_to_all x1, blocking collectives, local(): lax.all_to_all(jnp.stack(sending, axis=1), 'pix', 0, 0, tiled=True)  152 us
    all_to_all x2, waiting for transfers between devices, local(): lax.all_to_all(jnp.stack(sending, axis=1), 'pix', 0, 0, tiled=True)  82 us
    dot_general x8, matrix products, model_of(): jnp.dot(picked[b], pieces[c][b], precision=HIGHEST_PRECISION)  31.5 us
    dot_general x8, matrix products, outbound(): jnp.dot(centered[b], pieces[c][b].T, precision=HIGHEST_PRECISION)  30.9 us
    reduce_scatter x1, waiting for transfers between devices, local(): model_rows = lax.psum_scatter(term, 'mode', scatter_dimension=0, tiled=True)  19.9 us
    all_to_all x2, starting transfers between devices, local(): lax.all_to_all(jnp.stack(sending, axis=1), 'pix', 0, 0, tiled=True)  12.1 us
    ppermute x5, starting transfers between devices, butterfly_sum(): value = value + lax.ppermute(value, axes, pairs)  10.5 us
    dot_general x2, matrix products, inbound(): jnp.einsum('ba,bfk->afk', every_onehot, arrived.reshape(parts * blocks, r...  8.38 us
  transfers between devices with their start and end apart: 9, of which 8 were waited for; matrix products, arithmetic and copies ran while one was open for 10% of the time, Pallas kernels for 0%

commit v1 on v0

--- a/solution.py
+++ b/solution.py
@@ -57,9 +57,6 @@
     annulus_totals = packed[:, :total_frames]
     pixel_counts = packed[:, total_frames]
     every_onehot = packed[:, total_frames + 1 :].T
-    every_annulus = jnp.einsum(
-        "ba,a->b", every_onehot, jnp.arange(NA, dtype=jnp.float32), precision=HIGHEST_PRECISION
-    ).astype(jnp.int32)
     mode_ids = mode_index * modes_dev + jnp.arange(modes_dev, dtype=jnp.int32)
     retained = (mode_ids[None, :] < truncation[:, None]).astype(jnp.float32)
     annulus_means = annulus_totals / pixel_counts[:, None]
@@ -69,6 +66,8 @@
         for b in range(blocks)
     ]
     chunk = modes_dev // K_CHUNKS
+    same_annulus = jnp.einsum("ca,ba->cb", every_onehot, every_onehot, precision=HIGHEST_PRECISION)
+    block_retained = jnp.einsum("ba,ak->bk", every_onehot, retained, precision=HIGHEST_PRECISION)
     rows_dev = total_frames // parts
     pieces = [
         [
@@ -89,14 +88,13 @@
         return per_block.reshape(blocks, parts, rows_dev, chunk).transpose(1, 0, 2, 3)
 
     def inbound(c, arrived):
-        slice_coefficients = jnp.einsum(
-            "ba,bfk->afk",
-            every_onehot,
+        summed = jnp.einsum(
+            "cb,bfk->cfk",
+            same_annulus,
             arrived.reshape(parts * blocks, rows_dev, chunk),
             precision=HIGHEST_PRECISION,
         )
-        slice_truncated = slice_coefficients * retained[:, None, c * chunk : (c + 1) * chunk]
-        outgoing = jnp.take(slice_truncated, every_annulus, axis=0)
+        outgoing = summed * block_retained[:, None, c * chunk : (c + 1) * chunk]
         return outgoing.reshape(parts, blocks, rows_dev, chunk)
 
     def model_of(c, returned):

time: 413 us -> 409 us (level)
  other arithmetic: 19.9 us -> 13.7 us
    select_n x2 -> x0, other arithmetic: 6.17 us -> none  [inbound(): outgoing = jnp.take(slice_truncated, every_annulus, axis=0)]
    another operation x0 -> x2, local copies, waits for them, and re-layouts: none -> 5.33 us  [local(): jnp.stack(sending, axis=1)]
    gather x2 -> x0, local copies, waits for them, and re-layouts: 4.9 us -> none  [inbound(): outgoing = jnp.take(slice_truncated, every_annulus, axis=0)]
    dot_general x3 -> x4, matrix products: 8.58 us -> 12 us  [the longest x2 11.3 us: inbound(): jnp.einsum('cb,bfk->cfk', same_annulus, arrived.reshape(parts * blocks, r...]
where the time goes in v1:
time: 409 us; the launch traced here: 401 us
  blocking collectives  152 us (37%)
  waiting for transfers between devices  110 us (27%)
  matrix products  75 us (18%)
  starting transfers between devices  23.1 us (6%)
  between operations  14.2 us (3%)
  other arithmetic  13.7 us (3%)
  local copies, waits for them, and re-layouts  13.2 us (3%)
    all_to_all x1, blocking collectives, local(): lax.all_to_all(jnp.stack(sending, axis=1), 'pix', 0, 0, tiled=True)  152 us
    all_to_all x2, waiting for transfers between devices, local(): lax.all_to_all(jnp.stack(sending, axis=1), 'pix', 0, 0, tiled=True)  81.8 us
    dot_general x8, matrix products, model_of(): jnp.dot(picked[b], pieces[c][b], precision=HIGHEST_PRECISION)  31.7 us
    dot_general x8, matrix products, outbound(): jnp.dot(centered[b], pieces[c][b].T, precision=HIGHEST_PRECISION)  30.3 us
    reduce_scatter x1, waiting for transfers between devices, local(): model_rows = lax.psum_scatter(term, 'mode', scatter_dimension=0, tiled=True)  19.8 us
    all_to_all x2, starting transfers between devices, local(): lax.all_to_all(jnp.stack(sending, axis=1), 'pix', 0, 0, tiled=True)  12.4 us
    dot_general x2, matrix products, inbound(): jnp.einsum('cb,bfk->cfk', same_annulus, arrived.reshape(parts * blocks, r...  11.3 us
    ppermute x5, starting transfers between devices, butterfly_sum(): value = value + lax.ppermute(value, axes, pairs)  10.5 us
  transfers between devices with their start and end apart: 9, of which 8 were waited for; matrix products, arithmetic and copies ran while one was open for 10% of the time, Pallas kernels for 0%

profile of v1, /device:TPU:0, one launch (start us, length us, event | category | flops | bytes accessed | tf_op | source)
XLA Modules:
  0.0 401.3 jit_solution(9271519039345607301)
XLA Ops:
  28.0 4.1 %fusion.18 = f32[384,512]{1,0:T(8,128)S(1)} fusion(f32[1024,3072]{1,0:T(8,128)} %param.5, f32[384,3072]{1,0:T(8,128)} %all-gather.2.cloned.1.call-done, f32[384]{0:T(512)S(1)} %get-tuple-element.9), kind=kOutput, calls=%fused_computation.27 | convolution fusion | flops 1812234240 | bytes 3540480 | tf_op jit(solution)/shard_map/dot_general | solution.py:83
  32.0 3.9 fusion.14
  36.0 3.6 fusion.10
  39.6 3.6 fusion.6
  45.2 7.9 %all-to-all-start = ((f32[16,1,4,24,512]{4,3,2,1,0:T(8,128)}), f32[16,1,4,24,512]{4,3,2,1,0:T(8,128)}, u32[]{:S(2)}, u32[]{:S(2)}) async-start(f32[16,1,4,24,512]{4,3,2,1,0:T(8,128)} %maximum_bitcast_fusion.1), calls=%async_computation | async-start | bytes 6291456 | tf_op jit(solution)/shard_map/all_to_all | solution.py:115
  53.9 4.1 %fusion.34 = f32[384,512]{1,0:T(8,128)S(1)} fusion(f32[1024,3072]{1,0:T(8,128)} %param.5, f32[384,3072]{1,0:T(8,128)} %all-gather.2.cloned.1.call-done, f32[384]{0:T(512)S(1)} %get-tuple-element.9), kind=kOutput, calls=%fused_computation.43 | convolution fusion | flops 1812234240 | bytes 3540480 | tf_op jit(solution)/shard_map/dot_general | solution.py:83
  58.0 3.9 fusion.30
  62.0 3.6 fusion.26
  65.5 3.6 fusion.22
  71.1 41.2 %all-to-all-done = f32[16,1,4,24,512]{4,3,2,1,0:T(8,128)} async-done(((f32[16,1,4,24,512]{4,3,2,1,0:T(8,128)}), f32[16,1,4,24,512]{4,3,2,1,0:T(8,128)}, u32[]{:S(2)}, u32[]{:S(2)}) %all-to-all-start) | async-done | bytes 3145760 | tf_op jit(solution)/shard_map/all_to_all | solution.py:115
  112.3 6.7 %broadcast_multiply_fusion.1 = f32[64,24,512]{2,0,1:T(8,128)S(1)} fusion(f32[64,512]{1,0:T(8,128)S(1)} %get-tuple-element.28, f32[64,64,1]{1,0,2:T(8,128)S(1)} %convolution_bitcast_fusion, f32[64,24,512]{2,1,0:T(8,128)} %bitcast.30), kind=kOutput, calls=%fused_computation.12 | convolution fusion | flops 604766208 | bytes 6438912 | tf_op jit(solution)/shard_map/cb,bfk->cfk/dot_general | solution.py:91
  122.1 152.1 %all_to_all.15 = f32[16,2,4,24,512]{4,3,2,1,0:T(8,128)S(1)} all-to-all(f32[16,2,4,24,512]{4,3,2,1,0:T(8,128)S(1)} %pad_maximum_fusion), channel_id=1, replica_groups=mesh['pix'=16,'mode'=2] {'pix'}, dimensions={0} | all-to-all | bytes 12582912 | tf_op jit(solution)/shard_map/all_to_all | solution.py:115
  276.8 4.7 %broadcast_multiply_fusion = f32[64,24,512]{2,0,1:T(8,128)S(1)} fusion(f32[64,512]{1,0:T(8,128)S(1)} %get-tuple-element.27, f32[64,64,1]{1,0,2:T(8,128)S(1)} %convolution_bitcast_fusion, f32[64,24,512]{2,1,0:T(8,128)S(1)} %bitcast.80), kind=kOutput, calls=%fused_computation.11 | convolution fusion | flops 604766208 | bytes 6438912 | tf_op jit(solution)/shard_map/cb,bfk->cfk/dot_general | solution.py:91
  285.0 4.5 %all-to-all-start.2 = ((f32[16,1,4,24,512]{4,3,2,1,0:T(8,128)}), f32[16,1,4,24,512]{4,3,2,1,0:T(8,128)}, u32[]{:S(2)}, u32[]{:S(2)}) async-start(f32[16,1,4,24,512]{4,3,2,1,0:T(8,128)} %bitcast.78), calls=%async_computation.2 | async-start | bytes 6291456 | tf_op jit(solution)/shard_map/all_to_all | solution.py:115
  295.4 4.6 %fusion.16 = f32[384,768]{1,0:T(8,128)} fusion(f32[384,512]{1,0:T(8,128)S(1)} %bitcast.86, f32[1024,3072]{1,0:T(8,128)} %param.5), kind=kOutput, calls=%fused_computation.25 | convolution fusion | flops 1811939328 | bytes 3538944 | tf_op jit(solution)/shard_map/dot_general | solution.py:103
  300.0 4.5 %fusion.4 = f32[384,768]{1,0:T(8,128)} fusion(f32[384,512]{1,0:T(8,128)S(1)} %bitcast.84, f32[1024,3072]{1,0:T(8,128)} %param.5), kind=kOutput, calls=%fused_computation.13 | convolution fusion | flops 1811939328 | bytes 3538944 | tf_op jit(solution)/shard_map/dot_general | solution.py:103
  304.5 4.5 %fusion.8 = f32[384,768]{1,0:T(8,128)} fusion(f32[384,512]{1,0:T(8,128)S(1)} %bitcast.82, f32[1024,3072]{1,0:T(8,128)} %param.5), kind=kOutput, calls=%fused_computation.17 | convolution fusion | flops 1811939328 | bytes 3538944 | tf_op jit(solution)/shard_map/dot_general | solution.py:103
  309.0 40.5 %all-to-all-done.2 = f32[16,1,4,24,512]{4,3,2,1,0:T(8,128)} async-done(((f32[16,1,4,24,512]{4,3,2,1,0:T(8,128)}), f32[16,1,4,24,512]{4,3,2,1,0:T(8,128)}, u32[]{:S(2)}, u32[]{:S(2)}) %all-to-all-start.2) | async-done | bytes 3145760 | tf_op jit(solution)/shard_map/all_to_all | solution.py:115
  352.1 3.5 fusion.20
  355.7 3.5 fusion.24
  359.2 3.9 fusion.28
  363.2 3.5 fusion.32
  370.5 19.8 %reduce-scatter.2.cloned.1.call-done = f32[192,3072]{1,0:T(8,128)} async-done(((f32[384,3072]{1,0:T(8,128)}), f32[192,3072]{1,0:T(8,128)}) %reduce-scatter.2.cloned.1.call-update) | async-done | bytes 2359312 | tf_op jit(solution)/shard_map/reduce_scatter | solution.py:125
  390.3 3.6 maximum_subtract_fusion
  (71 shorter events, 47.5 us)
Async XLA Ops:
  6.5 1.7 copy-start
  6.5 1.9 copy-start.7
  6.5 21.4 %all-gather.2.cloned.1.call-start = ((), (), s32[]{:S(2)}) async-start(), calls=%async_computation.4 | async-start | bytes 7077888 | tf_op jit(solution)/shard_map/all_gather | solution.py:30
  9.3 1.3 collective-permute-start
  10.7 4.5 %collective-permute-start.1 = (f32[8,449]{1,0:T(8,128)S(1)}, f32[8,449]{1,0:T(8,128)S(1)}, u32[]{:S(2)}, u32[]{:S(2)}) collective-permute-start(f32[8,449]{1,0:T(8,128)S(1)} %fusion.82), channel_id=1, source_target_pairs={{0,2},{1,3},{2,0},{3,1},{4,6},{5,7},{6,4},{7,5},{8,10},{9,11},{10,... | collective-permute-start | bytes 43112 | tf_op jit(solution)/shard_map/ppermute | solution.py:17
  15.2 3.8 collective-permute-start.2
  19.0 3.8 collective-permute-start.3
  22.8 4.8 %collective-permute-start.4 = (f32[8,449]{1,0:T(8,128)S(1)}, f32[8,449]{1,0:T(8,128)S(1)}, u32[]{:S(2)}, u32[]{:S(2)}) collective-permute-start(f32[8,449]{1,0:T(8,128)S(1)} %add.60), channel_id=1, source_target_pairs={{0,16},{1,17},{2,18},{3,19},{4,20},{5,21},{6,22},{7,23},{8,24},{9,... | collective-permute-start | bytes 43112 | tf_op jit(solution)/shard_map/ppermute | solution.py:17
  28.0 8.0 %copy-start.1 = (f32[384,3072]{1,0:T(8,128)S(1)}, f32[384,3072]{1,0:T(8,128)}, u32[]{:S(2)}) copy-start(f32[384,3072]{1,0:T(8,128)} %all-gather.2.cloned.1.call-done) | copy-start | bytes 14155780
  45.2 8.3 %copy-start.6 = (s32[8]{0:T(128)S(1)}, s32[8]{0:T(128)}, u32[]{:S(2)}) copy-start(s32[8]{0:T(128)} %param.7) | copy-start | bytes 100
  45.2 16.7 %slice-start = ((s8[4718592]{0:T(1024)(128)(4,1)}), s8[524288]{0:T(1024)(128)(4,1)S(1)}, s32[]{:S(2)}) async-start(s8[4718592]{0:T(1024)(128)(4,1)} %bitcast.76), calls=%async_computation.6 | async-start | bytes 1048576
  45.2 67.1 %all-to-all-start = ((f32[16,1,4,24,512]{4,3,2,1,0:T(8,128)}), f32[16,1,4,24,512]{4,3,2,1,0:T(8,128)}, u32[]{:S(2)}, u32[]{:S(2)}) async-start(f32[16,1,4,24,512]{4,3,2,1,0:T(8,128)} %maximum_bitcast_fusion.1), calls=%async_computation | async-start | bytes 6291456 | tf_op jit(solution)/shard_map/all_to_all | solution.py:115
  53.9 8.1 %slice-start.1 = ((s8[4718592]{0:T(1024)(128)(4,1)}), s8[4194304]{0:T(1024)(128)(4,1)S(1)}, s32[]{:S(2)}) async-start(s8[4718592]{0:T(1024)(128)(4,1)} %bitcast.76), calls=%async_computation.7 | async-start | bytes 8388608
  119.0 1.9 copy-start.2
  285.0 64.6 %all-to-all-start.2 = ((f32[16,1,4,24,512]{4,3,2,1,0:T(8,128)}), f32[16,1,4,24,512]{4,3,2,1,0:T(8,128)}, u32[]{:S(2)}, u32[]{:S(2)}) async-start(f32[16,1,4,24,512]{4,3,2,1,0:T(8,128)} %bitcast.78), calls=%async_computation.2 | async-start | bytes 6291456 | tf_op jit(solution)/shard_map/all_to_all | solution.py:115
  289.5 100.9 %reduce-scatter.2.cloned.1.call-start = ((), (), s32[]{:S(2)}) async-start(), calls=%async_computation.5 | async-start | bytes 7077888 | tf_op jit(solution)/shard_map/reduce_scatter | solution.py:125
  359.2 7.5 %copy-start.3 = (f32[384,768]{1,0:T(8,128)S(1)}, f32[384,768]{1,0:T(8,128)}, u32[]{:S(2)}) copy-start(f32[384,768]{1,0:T(8,128)} %fusion.16) | copy-start | bytes 3538948
  359.2 7.5 %copy-start.4 = (f32[384,768]{1,0:T(8,128)S(1)}, f32[384,768]{1,0:T(8,128)}, u32[]{:S(2)}) copy-start(f32[384,768]{1,0:T(8,128)} %fusion.4) | copy-start | bytes 3538948
  359.2 7.5 %copy-start.5 = (f32[384,768]{1,0:T(8,128)S(1)}, f32[384,768]{1,0:T(8,128)}, u32[]{:S(2)}) copy-start(f32[384,768]{1,0:T(8,128)} %fusion.8) | copy-start | bytes 3538948
Sparse Core Ops, SparseCore 0:
  8.9 17.1 all-gather.1
  369.3 20.9 reduce-scatter.1

commit v2 on v1

--- a/solution.py
+++ b/solution.py
@@ -8,6 +8,7 @@
 
 
 HIGHEST_PRECISION = lax.Precision.HIGHEST
+PRODUCT_PRECISION = lax.Precision.HIGH
 
 
 def butterfly_sum(value, axes, size):
@@ -80,7 +81,7 @@
     def outbound(c):
         per_block = jnp.stack(
             [
-                jnp.dot(centered[b], pieces[c][b].T, precision=HIGHEST_PRECISION)
+                jnp.dot(centered[b], pieces[c][b].T, precision=PRODUCT_PRECISION)
                 for b in range(blocks)
             ],
             axis=0,
@@ -100,7 +101,7 @@
     def model_of(c, returned):
         picked = returned.transpose(1, 0, 2, 3).reshape(blocks, total_frames, chunk)
         return jnp.concatenate(
-            [jnp.dot(picked[b], pieces[c][b], precision=HIGHEST_PRECISION) for b in range(blocks)],
+            [jnp.dot(picked[b], pieces[c][b], precision=PRODUCT_PRECISION) for b in range(blocks)],
             axis=1,
         )
 

time: 409 us -> 393 us (0.961)
  the two profiles are of different devices: /device:TPU:0 before, /device:TPU:13 now
where the time goes in v2:
time: 393 us; the launch traced here: 392 us
  blocking collectives  141 us (36%)
  waiting for transfers between devices  135 us (34%)
  matrix products  59 us (15%)
  starting transfers between devices  16.4 us (4%)
  other arithmetic  13.7 us (3%)
  between operations  13.7 us (3%)
  local copies, waits for them, and re-layouts  13.2 us (3%)
    all_to_all x1, blocking collectives, local(): lax.all_to_all(jnp.stack(sending, axis=1), 'pix', 0, 0, tiled=True)  141 us
    all_to_all x2, waiting for transfers between devices, local(): lax.all_to_all(jnp.stack(sending, axis=1), 'pix', 0, 0, tiled=True)  111 us
    dot_general x8, matrix products, model_of(): jnp.dot(picked[b], pieces[c][b], precision=PRODUCT_PRECISION)  24.1 us
    dot_general x8, matrix products, outbound(): jnp.dot(centered[b], pieces[c][b].T, precision=PRODUCT_PRECISION)  22 us
    reduce_scatter x1, waiting for transfers between devices, local(): model_rows = lax.psum_scatter(term, 'mode', scatter_dimension=0, tiled=True)  11.7 us
    all_to_all x2, starting transfers between devices, local(): lax.all_to_all(jnp.stack(sending, axis=1), 'pix', 0, 0, tiled=True)  11.5 us
    dot_general x2, matrix products, inbound(): jnp.einsum('cb,bfk->cfk', same_annulus, arrived.reshape(parts * blocks, r...  11.1 us
    ppermute x5, waiting for transfers between devices, butterfly_sum(): value = value + lax.ppermute(value, axes, pairs)  8.18 us
  transfers between devices with their start and end apart: 9, of which 9 were waited for; matrix products, arithmetic and copies ran while one was open for 8% of the time, Pallas kernels for 0%

profile of v2, /device:TPU:13, one launch (start us, length us, event | category | flops | bytes accessed | tf_op | source)
XLA Modules:
  0.0 391.7 jit_solution(14741735206359090797)
XLA Ops:
  22.5 2.7 all-gather.2.cloned.1.call-done
  25.2 3.0 fusion.18
  28.3 2.9 fusion.14
  38.3 6.5 %all-to-all-start = ((f32[16,1,4,24,512]{4,3,2,1,0:T(8,128)}), f32[16,1,4,24,512]{4,3,2,1,0:T(8,128)}, u32[]{:S(2)}, u32[]{:S(2)}) async-start(f32[16,1,4,24,512]{4,3,2,1,0:T(8,128)} %maximum_bitcast_fusion.1), calls=%async_computation | async-start | bytes 6291456 | tf_op jit(solution)/shard_map/all_to_all | solution.py:116
  45.6 3.0 fusion.34
  48.7 2.9 fusion.30
  58.6 56.8 %all-to-all-done = f32[16,1,4,24,512]{4,3,2,1,0:T(8,128)} async-done(((f32[16,1,4,24,512]{4,3,2,1,0:T(8,128)}), f32[16,1,4,24,512]{4,3,2,1,0:T(8,128)}, u32[]{:S(2)}, u32[]{:S(2)}) %all-to-all-start) | async-done | bytes 3145760 | tf_op jit(solution)/shard_map/all_to_all | solution.py:116
  115.4 6.5 %broadcast_multiply_fusion.1 = f32[64,24,512]{2,0,1:T(8,128)S(1)} fusion(f32[64,512]{1,0:T(8,128)S(1)} %get-tuple-element.28, f32[64,64,1]{1,0,2:T(8,128)S(1)} %convolution_bitcast_fusion, f32[64,24,512]{2,1,0:T(8,128)} %bitcast.30), kind=kOutput, calls=%fused_computation.12 | convolution fusion | flops 604766208 | bytes 6438912 | tf_op jit(solution)/shard_map/cb,bfk->cfk/dot_general | solution.py:92
  125.0 141.3 %all_to_all.15 = f32[16,2,4,24,512]{4,3,2,1,0:T(8,128)S(1)} all-to-all(f32[16,2,4,24,512]{4,3,2,1,0:T(8,128)S(1)} %pad_maximum_fusion), channel_id=1, replica_groups=mesh['pix'=16,'mode'=2] {'pix'}, dimensions={0} | all-to-all | bytes 12582912 | tf_op jit(solution)/shard_map/all_to_all | solution.py:116
  266.2 2.6 fusion.67
  268.8 4.7 %broadcast_multiply_fusion = f32[64,24,512]{2,0,1:T(8,128)S(1)} fusion(f32[64,512]{1,0:T(8,128)S(1)} %get-tuple-element.27, f32[64,64,1]{1,0,2:T(8,128)S(1)} %convolution_bitcast_fusion, f32[64,24,512]{2,1,0:T(8,128)S(1)} %bitcast.80), kind=kOutput, calls=%fused_computation.11 | convolution fusion | flops 604766208 | bytes 6438912 | tf_op jit(solution)/shard_map/cb,bfk->cfk/dot_general | solution.py:92
  273.5 3.5 copy.45
  277.0 5.0 %all-to-all-start.2 = ((f32[16,1,4,24,512]{4,3,2,1,0:T(8,128)}), f32[16,1,4,24,512]{4,3,2,1,0:T(8,128)}, u32[]{:S(2)}, u32[]{:S(2)}) async-start(f32[16,1,4,24,512]{4,3,2,1,0:T(8,128)} %bitcast.78), calls=%async_computation.2 | async-start | bytes 6291456 | tf_op jit(solution)/shard_map/all_to_all | solution.py:116
  284.4 2.6 fusion.12
  287.1 3.7 fusion.16
  290.7 3.6 fusion.4
  294.3 3.6 fusion.8
  298.0 54.5 %all-to-all-done.2 = f32[16,1,4,24,512]{4,3,2,1,0:T(8,128)} async-done(((f32[16,1,4,24,512]{4,3,2,1,0:T(8,128)}), f32[16,1,4,24,512]{4,3,2,1,0:T(8,128)}, u32[]{:S(2)}, u32[]{:S(2)}) %all-to-all-start.2) | async-done | bytes 3145760 | tf_op jit(solution)/shard_map/all_to_all | solution.py:116
  355.0 2.6 fusion.20
  357.7 2.6 fusion.24
  360.3 2.8 fusion.28
  363.1 2.6 fusion.32
  369.5 11.7 %reduce-scatter.2.cloned.1.call-done = f32[192,3072]{1,0:T(8,128)} async-done(((f32[384,3072]{1,0:T(8,128)}), f32[192,3072]{1,0:T(8,128)}) %reduce-scatter.2.cloned.1.call-update) | async-done | bytes 2359312 | tf_op jit(solution)/shard_map/reduce_scatter | solution.py:126
  381.2 3.6 maximum_subtract_fusion
  (71 shorter events, 42.7 us)
Async XLA Ops:
  6.5 1.7 copy-start
  6.5 1.9 copy-start.7
  6.5 18.7 %all-gather.2.cloned.1.call-start = ((), (), s32[]{:S(2)}) async-start(), calls=%async_computation.4 | async-start | bytes 7077888 | tf_op jit(solution)/shard_map/all_gather | solution.py:31
  9.3 1.5 collective-permute-start
  10.9 2.6 collective-permute-start.1
  13.5 2.6 collective-permute-start.2
  16.1 2.6 collective-permute-start.3
  18.7 3.5 collective-permute-start.4
  25.2 5.9 %copy-start.1 = (f32[384,3072]{1,0:T(8,128)S(1)}, f32[384,3072]{1,0:T(8,128)}, u32[]{:S(2)}) copy-start(f32[384,3072]{1,0:T(8,128)} %all-gather.2.cloned.1.call-done) | copy-start | bytes 14155780
  38.3 6.9 %copy-start.6 = (s32[8]{0:T(128)S(1)}, s32[8]{0:T(128)}, u32[]{:S(2)}) copy-start(s32[8]{0:T(128)} %param.7) | copy-start | bytes 100
  38.3 13.2 %slice-start = ((s8[4718592]{0:T(1024)(128)(4,1)}), s8[524288]{0:T(1024)(128)(4,1)S(1)}, s32[]{:S(2)}) async-start(s8[4718592]{0:T(1024)(128)(4,1)} %bitcast.76), calls=%async_computation.6 | async-start | bytes 1048576
  38.3 77.1 %all-to-all-start = ((f32[16,1,4,24,512]{4,3,2,1,0:T(8,128)}), f32[16,1,4,24,512]{4,3,2,1,0:T(8,128)}, u32[]{:S(2)}, u32[]{:S(2)}) async-start(f32[16,1,4,24,512]{4,3,2,1,0:T(8,128)} %maximum_bitcast_fusion.1), calls=%async_computation | async-start | bytes 6291456 | tf_op jit(solution)/shard_map/all_to_all | solution.py:116
  45.6 6.0 %slice-start.1 = ((s8[4718592]{0:T(1024)(128)(4,1)}), s8[4194304]{0:T(1024)(128)(4,1)S(1)}, s32[]{:S(2)}) async-start(s8[4718592]{0:T(1024)(128)(4,1)} %bitcast.76), calls=%async_computation.7 | async-start | bytes 8388608
  121.9 1.9 copy-start.2
  277.0 75.5 %all-to-all-start.2 = ((f32[16,1,4,24,512]{4,3,2,1,0:T(8,128)}), f32[16,1,4,24,512]{4,3,2,1,0:T(8,128)}, u32[]{:S(2)}, u32[]{:S(2)}) async-start(f32[16,1,4,24,512]{4,3,2,1,0:T(8,128)} %bitcast.78), calls=%async_computation.2 | async-start | bytes 6291456 | tf_op jit(solution)/shard_map/all_to_all | solution.py:116
  282.0 99.2 %reduce-scatter.2.cloned.1.call-start = ((), (), s32[]{:S(2)}) async-start(), calls=%async_computation.5 | async-start | bytes 7077888 | tf_op jit(solution)/shard_map/reduce_scatter | solution.py:126
  360.3 5.4 %copy-start.3 = (f32[384,768]{1,0:T(8,128)S(1)}, f32[384,768]{1,0:T(8,128)}, u32[]{:S(2)}) copy-start(f32[384,768]{1,0:T(8,128)} %fusion.16) | copy-start | bytes 3538948
  360.3 5.4 %copy-start.4 = (f32[384,768]{1,0:T(8,128)S(1)}, f32[384,768]{1,0:T(8,128)}, u32[]{:S(2)}) copy-start(f32[384,768]{1,0:T(8,128)} %fusion.4) | copy-start | bytes 3538948
  360.3 5.4 %copy-start.5 = (f32[384,768]{1,0:T(8,128)S(1)}, f32[384,768]{1,0:T(8,128)}, u32[]{:S(2)}) copy-start(f32[384,768]{1,0:T(8,128)} %fusion.8) | copy-start | bytes 3538948
Sparse Core Ops, SparseCore 0:
  8.9 16.2 all-gather.1
  368.3 12.8 reduce-scatter.1

commit v3 on v2

--- a/solution.py
+++ b/solution.py
@@ -4,7 +4,6 @@
 from jax.sharding import PartitionSpec as P
 
 NA = 8
-K_CHUNKS = 2
 
 
 HIGHEST_PRECISION = lax.Precision.HIGHEST
@@ -66,19 +65,21 @@
         gathered[:, b * block_len : (b + 1) * block_len] - block_means[b][:, None]
         for b in range(blocks)
     ]
-    chunk = modes_dev // K_CHUNKS
     same_annulus = jnp.einsum("ca,ba->cb", every_onehot, every_onehot, precision=HIGHEST_PRECISION)
     block_retained = jnp.einsum("ba,ak->bk", every_onehot, retained, precision=HIGHEST_PRECISION)
     rows_dev = total_frames // parts
+    last = modes_dev // 4
+    bounds = [(0, modes_dev - last), (modes_dev - last, modes_dev)]
     pieces = [
-        [
-            basis[c * chunk : (c + 1) * chunk, b * block_len : (b + 1) * block_len]
-            for b in range(blocks)
-        ]
-        for c in range(K_CHUNKS)
+        [basis[lo:hi, b * block_len : (b + 1) * block_len] for b in range(blocks)]
+        for lo, hi in bounds
     ]
+    last_basis = lax.all_gather(basis[modes_dev - last :], "mode", axis=0, tiled=True).reshape(
+        groups, last, pix_dev
+    )
 
     def outbound(c):
+        width = bounds[c][1] - bounds[c][0]
         per_block = jnp.stack(
             [
                 jnp.dot(centered[b], pieces[c][b].T, precision=PRODUCT_PRECISION)
@@ -86,44 +87,54 @@
             ],
             axis=0,
         )
-        return per_block.reshape(blocks, parts, rows_dev, chunk).transpose(1, 0, 2, 3)
+        return per_block.reshape(blocks, parts, rows_dev, width).transpose(1, 0, 2, 3)
 
     def inbound(c, arrived):
+        lo, hi = bounds[c]
         summed = jnp.einsum(
             "cb,bfk->cfk",
             same_annulus,
-            arrived.reshape(parts * blocks, rows_dev, chunk),
+            arrived.reshape(parts * blocks, rows_dev, hi - lo),
             precision=HIGHEST_PRECISION,
         )
-        outgoing = summed * block_retained[:, None, c * chunk : (c + 1) * chunk]
-        return outgoing.reshape(parts, blocks, rows_dev, chunk)
+        outgoing = summed * block_retained[:, None, lo:hi]
+        return outgoing.reshape(parts, blocks, rows_dev, hi - lo)
 
-    def model_of(c, returned):
-        picked = returned.transpose(1, 0, 2, 3).reshape(blocks, total_frames, chunk)
-        return jnp.concatenate(
-            [jnp.dot(picked[b], pieces[c][b], precision=PRODUCT_PRECISION) for b in range(blocks)],
-            axis=1,
-        )
+    def picked_of(c, returned):
+        width = bounds[c][1] - bounds[c][0]
+        return returned.transpose(1, 0, 2, 3).reshape(blocks, total_frames, width)
 
-    term = None
-    pending = None
-    for stage in range(K_CHUNKS + 1):
-        sending = []
-        if stage < K_CHUNKS:
-            sending.append(outbound(stage))
-        if pending is not None:
-            sending.append(pending)
-        received = lax.all_to_all(jnp.stack(sending, axis=1), "pix", 0, 0, tiled=True)
-        slot = 0
-        next_pending = None
-        if stage < K_CHUNKS:
-            next_pending = inbound(stage, received[:, 0])
-            slot = 1
-        if pending is not None:
-            part = model_of(stage - 1, received[:, slot])
-            term = part if term is None else term + part
-        pending = next_pending
+    first_out = outbound(0)
+    arrived = lax.all_to_all(first_out, "pix", 0, 0, tiled=True)
+    pending = inbound(0, arrived)
+    second_out = outbound(1)
+    split = bounds[1][1] - bounds[1][0]
+    received = lax.all_to_all(
+        jnp.concatenate([second_out, pending], axis=3), "pix", 0, 0, tiled=True
+    )
+    pending = inbound(1, received[..., :split])
+    picked = picked_of(0, received[..., split:])
+    term = jnp.concatenate(
+        [jnp.dot(picked[b], pieces[0][b], precision=PRODUCT_PRECISION) for b in range(blocks)],
+        axis=1,
+    )
     model_rows = lax.psum_scatter(term, "mode", scatter_dimension=0, tiled=True)
+    returned = lax.all_to_all(pending, "pix", 0, 0, tiled=True)
+    picked = picked_of(1, returned).reshape(blocks, groups, own_rows, last)
+    picked = lax.all_to_all(picked, "mode", 1, 1, tiled=True)
+    last_model = jnp.concatenate(
+        [
+            jnp.einsum(
+                "mfk,mkp->fp",
+                picked[b],
+                last_basis[:, :, b * block_len : (b + 1) * block_len],
+                precision=PRODUCT_PRECISION,
+            )
+            for b in range(blocks)
+        ],
+        axis=1,
+    )
+    model_rows = model_rows + last_model
     own_means = lax.dynamic_slice_in_dim(block_means, mode_index * own_rows, own_rows, 1)
     own_centered = jnp.concatenate(
         [

time: 393 us -> 410 us (1.043)
  waiting for transfers between devices: 135 us -> 278 us
  blocking collectives: 141 us -> 0 us
  starting transfers between devices: 16.4 us -> 26.1 us
  local copies, waits for them, and re-layouts: 13.2 us -> 21.3 us
  matrix products: 59 us -> 54 us
    all_to_all x2 -> x4, waiting for transfers between devices: 111 us -> 266 us  [the longest x1 135 us: local(): lax.all_to_all(jnp.concatenate([second_out, pending], axis=3), 'pix', 0,...]
    all_to_all x1 -> x0, blocking collectives: 141 us -> none  [local(): lax.all_to_all(jnp.stack(sending, axis=1), 'pix', 0, 0, tiled=True)]
    reduce_scatter x1, waiting for transfers between devices: 11.7 us -> 0.01 us  [local(): model_rows = lax.psum_scatter(term, 'mode', scatter_dimension=0, tiled=True)]
    all_to_all x2 -> x4, starting transfers between devices: 11.5 us -> 21.2 us  [the longest x1 6.53 us: local(): arrived = lax.all_to_all(first_out, 'pix', 0, 0, tiled=True)]
    reshape x0 -> x3, local copies, waits for them, and re-layouts: none -> 8.55 us  [inbound(): return outgoing.reshape(parts, blocks, rows_dev, hi - lo)]
    concatenate x0 -> x2, other arithmetic: none -> 6.09 us  [the longest x1 3.39 us: local(): jnp.concatenate([second_out, pending], axis=3)]
    dot_general x8, matrix products: 24.1 us -> 18.7 us  [the longest x4 9.37 us: local(): jnp.einsum('mfk,mkp->fp', picked[b], last_basis[:, :, b * block_len:(b +...]
    another operation x3 -> x0, other arithmetic: 5.21 us -> none  [local(): jnp.stack(sending, axis=1)]
  transfers between devices with their start and end apart: 9 -> 12, of which waited for: 9 -> 10; matrix products, arithmetic and copies ran while one was open for 8% -> 14% of each run, Pallas kernels for 0% -> 0%
where the time goes in v3:
time: 410 us; the launch traced here: 409 us
  waiting for transfers between devices  278 us (68%)
  matrix products  54 us (13%)
  starting transfers between devices  26.1 us (6%)
  local copies, waits for them, and re-layouts  21.3 us (5%)
  other arithmetic  16.5 us (4%)
  between operations  13.4 us (3%)
    all_to_all x1, waiting for transfers between devices, local(): lax.all_to_all(jnp.concatenate([second_out, pending], axis=3), 'pix', 0,...  135 us
    all_to_all x1, waiting for transfers between devices, local(): arrived = lax.all_to_all(first_out, 'pix', 0, 0, tiled=True)  93.5 us
    all_to_all x1, waiting for transfers between devices, local(): returned = lax.all_to_all(pending, 'pix', 0, 0, tiled=True)  35.5 us
    dot_general x8, matrix products, outbound(): jnp.dot(centered[b], pieces[c][b].T, precision=PRODUCT_PRECISION)  22.6 us
    dot_general x2, matrix products, inbound(): jnp.einsum('cb,bfk->cfk', same_annulus, arrived.reshape(parts * blocks, r...  11 us
    dot_general x4, matrix products, local(): jnp.einsum('mfk,mkp->fp', picked[b], last_basis[:, :, b * block_len:(b +...  9.37 us
    dot_general x4, matrix products, local(): jnp.dot(picked[b], pieces[0][b], precision=PRODUCT_PRECISION)  9.35 us
    reshape x3, local copies, waits for them, and re-layouts, inbound(): return outgoing.reshape(parts, blocks, rows_dev, hi - lo)  8.55 us
  transfers between devices with their start and end apart: 12, of which 10 were waited for; matrix products, arithmetic and copies ran while one was open for 14% of the time, Pallas kernels for 0%

profile of v3, /device:TPU:13, one launch (start us, length us, event | category | flops | bytes accessed | tf_op | source)
XLA Modules:
  0.0 409.4 jit_solution(10207347524197836490)
XLA Ops:
  25.2 3.8 fusion.12
  29.0 3.3 fusion.8
  32.4 3.3 fusion.4
  35.7 3.3 fusion.16
  41.7 6.5 %all-to-all-start = ((f32[16,4,24,768]{3,2,1,0:T(8,128)}), f32[16,4,24,768]{3,2,1,0:T(8,128)}, u32[]{:S(2)}, u32[]{:S(2)}) async-start(f32[16,4,24,768]{3,2,1,0:T(8,128)} %maximum_bitcast_fusion), calls=%async_computation | async-start | bytes 9437184 | tf_op jit(solution)/shard_map/all_to_all | solution.py:108
  59.1 93.5 %all-to-all-done = f32[16,4,24,768]{3,2,1,0:T(8,128)} async-done(((f32[16,4,24,768]{3,2,1,0:T(8,128)}), f32[16,4,24,768]{3,2,1,0:T(8,128)}, u32[]{:S(2)}, u32[]{:S(2)}) %all-to-all-start) | async-done | bytes 4718624 | tf_op jit(solution)/shard_map/all_to_all | solution.py:108
  152.6 8.0 %broadcast_multiply_fusion = f32[64,24,768]{2,0,1:T(8,128)S(1)} fusion(f32[64,768]{1,0:T(8,128)S(1)} %slice-done.3, f32[64,64,1]{1,0,2:T(8,128)S(1)} %convolution_bitcast_fusion, f32[64,24,768]{2,1,0:T(8,128)} %bitcast.28), kind=kOutput, calls=%fused_computation.8 | convolution fusion | flops 907149312 | bytes 9650176 | tf_op jit(solution)/shard_map/cb,bfk->cfk/dot_general | solution.py:94
  160.7 2.7 copy.53
  163.4 3.4 pad_maximum_fusion
  166.8 4.6 %all-to-all-start.1 = ((f32[16,4,24,1024]{3,2,1,0:T(8,128)}), f32[16,4,24,1024]{3,2,1,0:T(8,128)}, u32[]{:S(2)}, u32[]{:S(2)}) async-start(f32[16,4,24,1024]{3,2,1,0:T(8,128)} %pad_maximum_fusion), calls=%async_computation.1 | async-start | bytes 12582912 | tf_op jit(solution)/shard_map/all_to_all | solution.py:112
  171.4 3.9 slice.176
  175.6 135.2 %all-to-all-done.1 = f32[16,4,24,1024]{3,2,1,0:T(8,128)} async-done(((f32[16,4,24,1024]{3,2,1,0:T(8,128)}), f32[16,4,24,1024]{3,2,1,0:T(8,128)}, u32[]{:S(2)}, u32[]{:S(2)}) %all-to-all-start.1) | async-done | bytes 6291488 | tf_op jit(solution)/shard_map/all_to_all | solution.py:112
  310.8 2.9 copy_bitcast_fusion
  314.1 4.1 %fusion.14 = f32[384,768]{1,0:T(8,128)S(1)} fusion(f32[384,768]{1,0:T(8,128)S(1)} %bitcast.101, f32[1024,3072]{1,0:T(8,128)} %param.5), kind=kOutput, calls=%fused_computation.21 | convolution fusion | flops 1358954496 | bytes 4718592 | tf_op jit(solution)/shard_map/dot_general | solution.py:118
  323.6 2.7 pad_maximum_fusion.1
  327.9 3.0 broadcast_multiply_fusion.1
  330.9 2.7 reshape.78
  333.6 3.1 copy.46
  336.7 5.0 %all-to-all-start.2 = ((f32[16,4,24,256]{3,1,2,0:T(4,128)}), f32[16,4,24,256]{3,1,2,0:T(4,128)}, u32[]{:S(2)}, u32[]{:S(2)}) async-start(f32[16,4,24,256]{3,1,2,0:T(4,128)} %copy.46), calls=%async_computation.3 | async-start | bytes 3145728 | tf_op jit(solution)/shard_map/all_to_all | solution.py:122
  343.4 35.5 %all-to-all-done.2 = f32[16,4,24,256]{3,1,2,0:T(4,128)} async-done(((f32[16,4,24,256]{3,1,2,0:T(4,128)}), f32[16,4,24,256]{3,1,2,0:T(4,128)}, u32[]{:S(2)}, u32[]{:S(2)}) %all-to-all-start.2) | async-done | bytes 1572896 | tf_op jit(solution)/shard_map/all_to_all | solution.py:122
  378.9 2.9 copy.47
  381.8 5.1 %all-to-all-start.3 = ((f32[4,2,192,256]{3,2,0,1:T(8,128)}), f32[4,2,192,256]{3,2,0,1:T(8,128)S(1)}, u32[]{:S(2)}, u32[]{:S(2)}) async-start(f32[4,2,192,256]{3,2,0,1:T(8,128)} %copy.47), calls=%async_computation.4 | async-start | bytes 3145728 | tf_op jit(solution)/shard_map/all_to_all | solution.py:124
  395.5 3.0 fusion.28
  398.6 4.3 %maximum_subtract_fusion = f32[192,3072]{1,0:T(8,128)} fusion(f32[192,768]{1,0:T(8,128)} %get-tuple-element.18, f32[192,768]{1,0:T(8,128)} %get-tuple-element.20, f32[192,768]{1,0:T(8,128)} %get-tuple-element.19, f32[192,768]{1,0:T(8,128)} %get-tuple-element.17, f32[192,3072]{1,0:T(8,128)} %reduce-scatter.2.cloned.1.call-done, f32[192,768]{1,0:T(8,128)S(1)} %fusion.37, ...), kind=kLoop, calls=%fused_computation.6 | loop fusion | flops 4718592 | bytes 9437184 | tf_op jit(solution)/shard_map/sub | solution.py:146
  (80 shorter events, 50.0 us)
Async XLA Ops:
  6.5 1.7 copy-start
  6.5 0.8 copy-start.5
  6.5 18.7 %all-gather.3.cloned.1.call-start = ((), (), s32[]{:S(2)}) async-start(), calls=%async_computation.5 | async-start | bytes 7077888 | tf_op jit(solution)/shard_map/all_gather | solution.py:30
  9.3 1.5 collective-permute-start
  10.9 2.6 collective-permute-start.1
  13.5 2.6 collective-permute-start.2
  16.1 2.6 collective-permute-start.3
  18.7 3.5 collective-permute-start.4
  25.2 3.8 copy-start.1
  41.7 6.5 %copy-start.4 = (s32[8]{0:T(128)S(1)}, s32[8]{0:T(128)}, u32[]{:S(2)}) copy-start(s32[8]{0:T(128)} %param.7) | copy-start | bytes 100
  41.7 110.9 %all-to-all-start = ((f32[16,4,24,768]{3,2,1,0:T(8,128)}), f32[16,4,24,768]{3,2,1,0:T(8,128)}, u32[]{:S(2)}, u32[]{:S(2)}) async-start(f32[16,4,24,768]{3,2,1,0:T(8,128)} %maximum_bitcast_fusion), calls=%async_computation | async-start | bytes 9437184 | tf_op jit(solution)/shard_map/all_to_all | solution.py:108
  48.6 4.7 %copy-start.3 = (f32[64,1024]{1,0:T(8,128)}, f32[64,1024]{1,0:T(8,128)S(1)}, u32[]{:S(2)}) copy-start(f32[64,1024]{1,0:T(8,128)S(1)} %fusion.58) | copy-start | bytes 786436
  55.6 97.1 %slice-start.3 = ((f32[64,1024]{1,0:T(8,128)}), f32[64,768]{1,0:T(8,128)S(1)}, s32[]{:S(2)}) async-start(f32[64,1024]{1,0:T(8,128)} %copy-done.3), calls=%async_computation.11 | async-start | bytes 393216 | tf_op jit(solution)/shard_map/slice | solution.py:100
  160.7 2.8 copy-start.2
  166.8 144.0 %all-to-all-start.1 = ((f32[16,4,24,1024]{3,2,1,0:T(8,128)}), f32[16,4,24,1024]{3,2,1,0:T(8,128)}, u32[]{:S(2)}, u32[]{:S(2)}) async-start(f32[16,4,24,1024]{3,2,1,0:T(8,128)} %pad_maximum_fusion), calls=%async_computation.1 | async-start | bytes 12582912 | tf_op jit(solution)/shard_map/all_to_all | solution.py:112
  171.4 215.5 %all-gather.5.cloned.1.call-start = ((), (), s32[]{:S(2)}) async-start(), calls=%async_computation.7 | async-start | bytes 9437184 | tf_op jit(solution)/shard_map/all_gather | solution.py:77
  175.4 223.2 %reduce-scatter.2.cloned.1.call-start = ((), (), s32[]{:S(2)}) async-start(), calls=%async_computation.6 | async-start | bytes 7077888 | tf_op jit(solution)/shard_map/reduce_scatter | solution.py:121
  310.8 7.5 %slice-start = ((s8[12582912]{0:T(1024)(128)(4,1)}), s8[4194304]{0:T(1024)(128)(4,1)S(1)}, s32[]{:S(2)}) async-start(s8[12582912]{0:T(1024)(128)(4,1)} %bitcast.90), calls=%async_computation.8 | async-start | bytes 8388608
  310.8 7.5 %slice-start.1 = ((s8[12582912]{0:T(1024)(128)(4,1)}), s8[4194304]{0:T(1024)(128)(4,1)S(1)}, s32[]{:S(2)}) async-start(s8[12582912]{0:T(1024)(128)(4,1)} %bitcast.90), calls=%async_computation.9 | async-start | bytes 8388608
  313.7 4.6 %slice-start.2 = ((s8[12582912]{0:T(1024)(128)(4,1)}), s8[4194304]{0:T(1024)(128)(4,1)S(1)}, s32[]{:S(2)}) async-start(s8[12582912]{0:T(1024)(128)(4,1)} %bitcast.90), calls=%async_computation.10 | async-start | bytes 8388608
  326.3 1.6 slice-start.4
  336.7 42.2 %all-to-all-start.2 = ((f32[16,4,24,256]{3,1,2,0:T(4,128)}), f32[16,4,24,256]{3,1,2,0:T(4,128)}, u32[]{:S(2)}, u32[]{:S(2)}) async-start(f32[16,4,24,256]{3,1,2,0:T(4,128)} %copy.46), calls=%async_computation.3 | async-start | bytes 3145728 | tf_op jit(solution)/shard_map/all_to_all | solution.py:122
  381.8 7.4 %all-to-all-start.3 = ((f32[4,2,192,256]{3,2,0,1:T(8,128)}), f32[4,2,192,256]{3,2,0,1:T(8,128)S(1)}, u32[]{:S(2)}, u32[]{:S(2)}) async-start(f32[4,2,192,256]{3,2,0,1:T(8,128)} %copy.47), calls=%async_computation.4 | async-start | bytes 3145728 | tf_op jit(solution)/shard_map/all_to_all | solution.py:124
Sparse Core Ops, SparseCore 0:
  8.9 16.2 all-gather.2
  175.5 19.3 all-gather.4
  326.4 13.8 reduce-scatter.1

commit v4 on v2

--- a/solution.py
+++ b/solution.py
@@ -12,11 +12,25 @@
 
 
 def butterfly_sum(value, axes, size):
-    step = 1
-    while step < size:
-        pairs = [(i, i ^ step) for i in range(size)]
-        value = value + lax.ppermute(value, axes, pairs)
-        step *= 2
+    index = lax.axis_index(axes)
+    stride = 1
+    while stride < size:
+        radix = 4 if (size // stride) % 4 == 0 else 2
+        digit = (index // stride) % radix
+        arrived = [value]
+        for shift in range(1, radix):
+            pairs = []
+            for i in range(size):
+                d = (i // stride) % radix
+                pairs.append((i, i + (((d + shift) % radix) - d) * stride))
+            arrived.append(lax.ppermute(value, axes, pairs))
+        stacked = jnp.stack(arrived, axis=0)
+        total = None
+        for member in range(radix):
+            picked = stacked[(digit - member) % radix]
+            total = picked if total is None else total + picked
+        value = total
+        stride *= radix
     return value
 
 
@@ -79,14 +93,15 @@
     ]
 
     def outbound(c):
-        per_block = jnp.stack(
+        return jnp.stack(
             [
-                jnp.dot(centered[b], pieces[c][b].T, precision=PRODUCT_PRECISION)
+                jnp.dot(centered[b], pieces[c][b].T, precision=PRODUCT_PRECISION).reshape(
+                    parts, rows_dev, chunk
+                )
                 for b in range(blocks)
             ],
-            axis=0,
+            axis=1,
         )
-        return per_block.reshape(blocks, parts, rows_dev, chunk).transpose(1, 0, 2, 3)
 
     def inbound(c, arrived):
         summed = jnp.einsum(

time: 393 us -> 400 us (1.018); the launches traced: 392 us -> 393 us
    ppermute x5 -> x7, waiting for transfers between devices: 8.18 us -> 7.25 us  [butterfly_sum(): arrived.append(lax.ppermute(value, axes, pairs))]
  transfers between devices with their start and end apart: 9 -> 11, of which waited for: 9 -> 11; matrix products, arithmetic and copies ran while one was open for 8% -> 8% of each run, Pallas kernels for 0% -> 0%
where the time goes in v4:
time: 400 us; the launch traced here: 393 us
  blocking collectives  142 us (36%)
  waiting for transfers between devices  133 us (33%)
  matrix products  59 us (15%)
  starting transfers between devices  18.6 us (5%)
  between operations  14 us (4%)
  other arithmetic  13.7 us (3%)
  local copies, waits for them, and re-layouts  13.1 us (3%)
    all_to_all x1, blocking collectives, local(): lax.all_to_all(jnp.stack(sending, axis=1), 'pix', 0, 0, tiled=True)  142 us
    all_to_all x2, waiting for transfers between devices, local(): lax.all_to_all(jnp.stack(sending, axis=1), 'pix', 0, 0, tiled=True)  111 us
    dot_general x8, matrix products, model_of(): jnp.dot(picked[b], pieces[c][b], precision=PRODUCT_PRECISION)  24.1 us
    dot_general x8, matrix products, outbound(): jnp.dot(centered[b], pieces[c][b].T, precision=PRODUCT_PRECISION)  22 us
    all_to_all x2, starting transfers between devices, local(): lax.all_to_all(jnp.stack(sending, axis=1), 'pix', 0, 0, tiled=True)  12.1 us
    reduce_scatter x1, waiting for transfers between devices, local(): model_rows = lax.psum_scatter(term, 'mode', scatter_dimension=0, tiled=True)  11.7 us
    dot_general x2, matrix products, inbound(): jnp.einsum('cb,bfk->cfk', same_annulus, arrived.reshape(parts * blocks, r...  11.1 us
  transfers between devices with their start and end apart: 11, of which 11 were waited for; matrix products, arithmetic and copies ran while one was open for 8% of the time, Pallas kernels for 0%

profile of v4, /device:TPU:13, one launch (start us, length us, event | category | flops | bytes accessed | tf_op | source)
XLA Modules:
  0.0 393.1 jit_solution(4249898998415570305)
XLA Ops:
  25.2 3.0 fusion.24
  28.3 2.9 fusion.20
  31.2 2.5 fusion.16
  38.3 7.1 %all-to-all-start = ((f32[16,1,4,24,512]{4,3,2,1,0:T(8,128)}), f32[16,1,4,24,512]{4,3,2,1,0:T(8,128)}, u32[]{:S(2)}, u32[]{:S(2)}) async-start(f32[16,1,4,24,512]{4,3,2,1,0:T(8,128)} %maximum_bitcast_fusion.1), calls=%async_computation | async-start | bytes 6291456 | tf_op jit(solution)/shard_map/all_to_all | solution.py:131
  46.3 3.0 fusion.40
  49.3 2.9 fusion.36
  59.3 56.4 %all-to-all-done = f32[16,1,4,24,512]{4,3,2,1,0:T(8,128)} async-done(((f32[16,1,4,24,512]{4,3,2,1,0:T(8,128)}), f32[16,1,4,24,512]{4,3,2,1,0:T(8,128)}, u32[]{:S(2)}, u32[]{:S(2)}) %all-to-all-start) | async-done | bytes 3145760 | tf_op jit(solution)/shard_map/all_to_all | solution.py:131
  115.7 6.5 %fusion.4 = f32[64,24,512]{2,0,1:T(8,128)S(1)} fusion(f32[64,64,1]{1,0,2:T(8,128)S(1)} %convolution_bitcast_fusion, f32[64,24,512]{2,1,0:T(8,128)} %bitcast.39, f32[64,512]{1,0:T(8,128)S(1)} %get-tuple-element.28), kind=kOutput, calls=%fused_computation.11 | convolution fusion | flops 604766208 | bytes 6438912 | tf_op jit(solution)/shard_map/cb,bfk->cfk/dot_general | solution.py:107
  125.3 142.1 %all_to_all.15 = f32[16,2,4,24,512]{4,3,2,1,0:T(8,128)S(1)} all-to-all(f32[16,2,4,24,512]{4,3,2,1,0:T(8,128)S(1)} %pad_maximum_fusion), channel_id=1, replica_groups=mesh['pix'=16,'mode'=2] {'pix'}, dimensions={0} | all-to-all | bytes 12582912 | tf_op jit(solution)/shard_map/all_to_all | solution.py:131
  267.4 2.6 fusion.77
  270.0 4.7 %fusion.7 = f32[64,24,512]{2,0,1:T(8,128)S(1)} fusion(f32[64,64,1]{1,0,2:T(8,128)S(1)} %convolution_bitcast_fusion, f32[64,24,512]{2,1,0:T(8,128)S(1)} %bitcast.91, f32[64,512]{1,0:T(8,128)S(1)} %get-tuple-element.27), kind=kOutput, calls=%fused_computation.12 | convolution fusion | flops 604766208 | bytes 6438912 | tf_op jit(solution)/shard_map/cb,bfk->cfk/dot_general | solution.py:107
  274.6 3.5 copy.45
  278.1 5.0 %all-to-all-start.2 = ((f32[16,1,4,24,512]{4,3,2,1,0:T(8,128)}), f32[16,1,4,24,512]{4,3,2,1,0:T(8,128)}, u32[]{:S(2)}, u32[]{:S(2)}) async-start(f32[16,1,4,24,512]{4,3,2,1,0:T(8,128)} %bitcast.89), calls=%async_computation.2 | async-start | bytes 6291456 | tf_op jit(solution)/shard_map/all_to_all | solution.py:131
  285.5 2.6 fusion.10
  288.1 3.6 fusion.14
  291.7 3.6 fusion.18
  295.3 3.7 fusion.22
  299.0 54.6 %all-to-all-done.2 = f32[16,1,4,24,512]{4,3,2,1,0:T(8,128)} async-done(((f32[16,1,4,24,512]{4,3,2,1,0:T(8,128)}), f32[16,1,4,24,512]{4,3,2,1,0:T(8,128)}, u32[]{:S(2)}, u32[]{:S(2)}) %all-to-all-start.2) | async-done | bytes 3145760 | tf_op jit(solution)/shard_map/all_to_all | solution.py:131
  356.1 2.6 fusion.26
  358.8 2.6 fusion.30
  361.4 2.8 fusion.34
  364.2 2.6 fusion.38
  370.6 11.7 %reduce-scatter.2.cloned.1.call-done = f32[192,3072]{1,0:T(8,128)} async-done(((f32[384,3072]{1,0:T(8,128)}), f32[192,3072]{1,0:T(8,128)}) %reduce-scatter.2.cloned.1.call-update) | async-done | bytes 2359312 | tf_op jit(solution)/shard_map/reduce_scatter | solution.py:141
  382.3 3.6 maximum_subtract_fusion
  (78 shorter events, 42.7 us)
Async XLA Ops:
  6.5 1.7 copy-start
  6.5 1.9 copy-start.7
  6.5 18.7 %all-gather.2.cloned.1.call-start = ((), (), s32[]{:S(2)}) async-start(), calls=%async_computation.4 | async-start | bytes 7077888 | tf_op jit(solution)/shard_map/all_gather | solution.py:45
  9.3 2.6 collective-permute-start
  11.1 2.6 collective-permute-start.1
  11.3 3.2 collective-permute-start.2
  14.5 2.6 collective-permute-start.3
  14.6 2.7 collective-permute-start.4
  16.0 3.5 collective-permute-start.5
  19.5 3.6 collective-permute-start.6
  25.2 5.9 %copy-start.1 = (f32[384,3072]{1,0:T(8,128)S(1)}, f32[384,3072]{1,0:T(8,128)}, u32[]{:S(2)}) copy-start(f32[384,3072]{1,0:T(8,128)} %all-gather.2.cloned.1.call-done) | copy-start | bytes 14155780
  38.3 7.5 %copy-start.6 = (s32[8]{0:T(128)S(1)}, s32[8]{0:T(128)}, u32[]{:S(2)}) copy-start(s32[8]{0:T(128)} %param.7) | copy-start | bytes 100
  38.3 13.9 %slice-start = ((s8[4718592]{0:T(1024)(128)(4,1)}), s8[524288]{0:T(1024)(128)(4,1)S(1)}, s32[]{:S(2)}) async-start(s8[4718592]{0:T(1024)(128)(4,1)} %bitcast.87), calls=%async_computation.6 | async-start | bytes 1048576
  38.3 77.4 %all-to-all-start = ((f32[16,1,4,24,512]{4,3,2,1,0:T(8,128)}), f32[16,1,4,24,512]{4,3,2,1,0:T(8,128)}, u32[]{:S(2)}, u32[]{:S(2)}) async-start(f32[16,1,4,24,512]{4,3,2,1,0:T(8,128)} %maximum_bitcast_fusion.1), calls=%async_computation | async-start | bytes 6291456 | tf_op jit(solution)/shard_map/all_to_all | solution.py:131
  46.2 6.0 %slice-start.1 = ((s8[4718592]{0:T(1024)(128)(4,1)}), s8[4194304]{0:T(1024)(128)(4,1)S(1)}, s32[]{:S(2)}) async-start(s8[4718592]{0:T(1024)(128)(4,1)} %bitcast.87), calls=%async_computation.7 | async-start | bytes 8388608
  122.2 1.9 copy-start.2
  278.1 75.5 %all-to-all-start.2 = ((f32[16,1,4,24,512]{4,3,2,1,0:T(8,128)}), f32[16,1,4,24,512]{4,3,2,1,0:T(8,128)}, u32[]{:S(2)}, u32[]{:S(2)}) async-start(f32[16,1,4,24,512]{4,3,2,1,0:T(8,128)} %bitcast.89), calls=%async_computation.2 | async-start | bytes 6291456 | tf_op jit(solution)/shard_map/all_to_all | solution.py:131
  283.1 99.3 %reduce-scatter.2.cloned.1.call-start = ((), (), s32[]{:S(2)}) async-start(), calls=%async_computation.5 | async-start | bytes 7077888 | tf_op jit(solution)/shard_map/reduce_scatter | solution.py:141
  361.4 5.4 %copy-start.3 = (f32[384,768]{1,0:T(8,128)S(1)}, f32[384,768]{1,0:T(8,128)}, u32[]{:S(2)}) copy-start(f32[384,768]{1,0:T(8,128)} %fusion.14) | copy-start | bytes 3538948
  361.4 5.4 %copy-start.4 = (f32[384,768]{1,0:T(8,128)S(1)}, f32[384,768]{1,0:T(8,128)}, u32[]{:S(2)}) copy-start(f32[384,768]{1,0:T(8,128)} %fusion.18) | copy-start | bytes 3538948
  361.4 5.4 %copy-start.5 = (f32[384,768]{1,0:T(8,128)S(1)}, f32[384,768]{1,0:T(8,128)}, u32[]{:S(2)}) copy-start(f32[384,768]{1,0:T(8,128)} %fusion.22) | copy-start | bytes 3538948
Sparse Core Ops, SparseCore 0:
  8.9 16.2 all-gather.1
  369.4 12.8 reduce-scatter.1

commit v5 on v2

--- a/solution.py
+++ b/solution.py
@@ -98,10 +98,23 @@
         outgoing = summed * block_retained[:, None, c * chunk : (c + 1) * chunk]
         return outgoing.reshape(parts, blocks, rows_dev, chunk)
 
+    whole_basis = lax.all_gather(basis, "mode", axis=0, tiled=True).reshape(
+        groups, modes_dev, pix_dev
+    )
+
     def model_of(c, returned):
-        picked = returned.transpose(1, 0, 2, 3).reshape(blocks, total_frames, chunk)
+        picked = returned.transpose(1, 0, 2, 3).reshape(blocks, groups, own_rows, chunk)
+        picked = lax.all_to_all(picked, "mode", 1, 1, tiled=True)
         return jnp.concatenate(
-            [jnp.dot(picked[b], pieces[c][b], precision=PRODUCT_PRECISION) for b in range(blocks)],
+            [
+                jnp.einsum(
+                    "mfk,mkp->fp",
+                    picked[b],
+                    whole_basis[:, c * chunk : (c + 1) * chunk, b * block_len : (b + 1) * block_len],
+                    precision=PRODUCT_PRECISION,
+                )
+                for b in range(blocks)
+            ],
             axis=1,
         )
 
@@ -123,7 +136,7 @@
             part = model_of(stage - 1, received[:, slot])
             term = part if term is None else term + part
         pending = next_pending
-    model_rows = lax.psum_scatter(term, "mode", scatter_dimension=0, tiled=True)
+    model_rows = term
     own_means = lax.dynamic_slice_in_dim(block_means, mode_index * own_rows, own_rows, 1)
     own_centered = jnp.concatenate(
         [

time: 393 us -> 405 us (1.031)
  blocking collectives: 141 us -> 157 us
  waiting for transfers between devices: 135 us -> 124 us
  matrix products: 59 us -> 64.3 us
  local copies, waits for them, and re-layouts: 13.2 us -> 17.8 us
    all_to_all x0 -> x2, blocking collectives: none -> 15.9 us  [model_of(): picked = lax.all_to_all(picked, 'mode', 1, 1, tiled=True)]
    reduce_scatter x1 -> x0, waiting for transfers between devices: 11.7 us -> none  [local(): model_rows = lax.psum_scatter(term, 'mode', scatter_dimension=0, tiled=True)]
    another operation x2 -> x3, local copies, waits for them, and re-layouts: 5.33 us -> 11.2 us  [local(): jnp.stack(sending, axis=1)]
  transfers between devices with their start and end apart: 9 -> 9, of which waited for: 9 -> 8; matrix products, arithmetic and copies ran while one was open for 8% -> 19% of each run, Pallas kernels for 0% -> 0%
where the time goes in v5:
time: 405 us; the launch traced here: 403 us
  blocking collectives  157 us (39%)
  waiting for transfers between devices  124 us (31%)
  matrix products  64.3 us (16%)
  local copies, waits for them, and re-layouts  17.8 us (4%)
  starting transfers between devices  16.5 us (4%)
  between operations  13.7 us (3%)
  other arithmetic  10 us (2%)
    all_to_all x1, blocking collectives, local(): lax.all_to_all(jnp.stack(sending, axis=1), 'pix', 0, 0, tiled=True)  141 us
    all_to_all x2, waiting for transfers between devices, local(): lax.all_to_all(jnp.stack(sending, axis=1), 'pix', 0, 0, tiled=True)  112 us
    dot_general x8, matrix products, model_of(): jnp.einsum('mfk,mkp->fp', picked[b], whole_basis[:, c * chunk:(c + 1) * c...  26 us
    dot_general x8, matrix products, outbound(): jnp.dot(centered[b], pieces[c][b].T, precision=PRODUCT_PRECISION)  24 us
    all_to_all x2, blocking collectives, model_of(): picked = lax.all_to_all(picked, 'mode', 1, 1, tiled=True)  15.9 us
    dot_general x2, matrix products, inbound(): jnp.einsum('cb,bfk->cfk', same_annulus, arrived.reshape(parts * blocks, r...  12.7 us
    all_to_all x2, starting transfers between devices, local(): lax.all_to_all(jnp.stack(sending, axis=1), 'pix', 0, 0, tiled=True)  11.8 us
    another operation x3, local copies, waits for them, and re-layouts, local(): jnp.stack(sending, axis=1)  11.2 us
  transfers between devices with their start and end apart: 9, of which 8 were waited for; matrix products, arithmetic and copies ran while one was open for 19% of the time, Pallas kernels for 0%

profile of v5, /device:TPU:13, one launch (start us, length us, event | category | flops | bytes accessed | tf_op | source)
XLA Modules:
  0.0 402.9 jit_solution(2906154922797418362)
XLA Ops:
  25.2 3.0 fusion.26
  33.7 2.9 fusion.20
  39.4 6.5 %all-to-all-start = ((f32[16,1,4,24,512]{4,3,2,1,0:T(8,128)}), f32[16,1,4,24,512]{4,3,2,1,0:T(8,128)}, u32[]{:S(2)}, u32[]{:S(2)}) async-start(f32[16,1,4,24,512]{4,3,2,1,0:T(8,128)} %maximum_bitcast_fusion.1), calls=%async_computation | async-start | bytes 6291456 | tf_op jit(solution)/shard_map/all_to_all | solution.py:129
  46.7 3.5 fusion.34
  50.2 3.5 fusion.32
  53.8 3.0 fusion.30
  61.4 55.1 %all-to-all-done = f32[16,1,4,24,512]{4,3,2,1,0:T(8,128)} async-done(((f32[16,1,4,24,512]{4,3,2,1,0:T(8,128)}), f32[16,1,4,24,512]{4,3,2,1,0:T(8,128)}, u32[]{:S(2)}, u32[]{:S(2)}) %all-to-all-start) | async-done | bytes 3145760 | tf_op jit(solution)/shard_map/all_to_all | solution.py:129
  116.5 6.5 %broadcast_multiply_fusion.1 = f32[64,24,512]{2,0,1:T(8,128)S(1)} fusion(f32[64,512]{1,0:T(8,128)S(1)} %get-tuple-element.20, f32[64,64,1]{1,0,2:T(8,128)S(1)} %convolution_bitcast_fusion, f32[64,24,512]{2,1,0:T(8,128)} %bitcast.30), kind=kOutput, calls=%fused_computation.26 | convolution fusion | flops 604766208 | bytes 6438912 | tf_op jit(solution)/shard_map/cb,bfk->cfk/dot_general | solution.py:92
  126.1 141.1 %all_to_all.25 = f32[16,2,4,24,512]{4,3,2,1,0:T(8,128)S(1)} all-to-all(f32[16,2,4,24,512]{4,3,2,1,0:T(8,128)S(1)} %pad_maximum_fusion), channel_id=1, replica_groups=mesh['pix'=16,'mode'=2] {'pix'}, dimensions={0} | all-to-all | bytes 12582912 | tf_op jit(solution)/shard_map/all_to_all | solution.py:129
  269.8 6.2 %broadcast_multiply_fusion = f32[64,24,512]{2,0,1:T(8,128)} fusion(f32[64,512]{1,0:T(8,128)S(1)} %get-tuple-element.19, f32[64,64,1]{1,0,2:T(8,128)S(1)} %convolution_bitcast_fusion, f32[64,24,512]{2,1,0:T(8,128)S(1)} %bitcast.130), kind=kOutput, calls=%fused_computation.25 | convolution fusion | flops 604766208 | bytes 6438912 | tf_op jit(solution)/shard_map/cb,bfk->cfk/dot_general | solution.py:92
  276.1 4.8 %stack_reshape.7 = f32[16,1,4,24,512]{4,2,0,3,1:T(4,128)} reshape(f32[64,24,512]{2,0,1:T(8,128)} %broadcast_multiply_fusion) | data formatting | bytes 6291456 | tf_op jit(solution)/shard_map/stack;reshape | solution.py:129
  280.9 4.6 %copy.79 = f32[16,1,4,24,512]{4,2,3,1,0:T(4,128)} copy(f32[16,1,4,24,512]{4,2,0,3,1:T(4,128)} %stack_reshape.7) | data formatting | bytes 6291456 | tf_op jit(solution)/shard_map/stack;reshape | solution.py:129
  286.1 8.8 %all_to_all.26 = f32[4,2,192,512]{3,2,0,1:T(8,128)} all-to-all(f32[4,2,192,512]{3,2,0,1:T(8,128)S(1)} %copy.73), channel_id=1, replica_groups=mesh['pix'=16,'mode'=2] {'mode'}, dimensions={1} | all-to-all | bytes 6291456 | tf_op jit(solution)/shard_map/all_to_all | solution.py:107
  294.9 5.3 %all-to-all-start.3 = ((f32[16,1,4,24,512]{4,2,3,1,0:T(4,128)}), f32[16,1,4,24,512]{4,2,3,1,0:T(4,128)}, u32[]{:S(2)}, u32[]{:S(2)}) async-start(f32[16,1,4,24,512]{4,2,3,1,0:T(4,128)} %copy.79), calls=%async_computation.3 | async-start | bytes 6291456 | tf_op jit(solution)/shard_map/all_to_all | solution.py:129
  301.4 3.5 fusion.36
  305.0 3.2 fusion.39
  308.2 3.2 fusion.42
  311.4 3.2 fusion.45
  314.6 57.0 %all-to-all-done.3 = f32[16,1,4,24,512]{4,2,3,1,0:T(4,128)} async-done(((f32[16,1,4,24,512]{4,2,3,1,0:T(4,128)}), f32[16,1,4,24,512]{4,2,3,1,0:T(4,128)}, u32[]{:S(2)}, u32[]{:S(2)}) %all-to-all-start.3) | async-done | bytes 3145760 | tf_op jit(solution)/shard_map/all_to_all | solution.py:129
  374.4 7.1 %all_to_all.27 = f32[4,2,192,512]{3,2,0,1:T(8,128)S(1)} all-to-all(f32[4,2,192,512]{3,2,0,1:T(8,128)S(1)} %copy.80), channel_id=1, replica_groups=mesh['pix'=16,'mode'=2] {'mode'}, dimensions={1} | all-to-all | bytes 6291456 | tf_op jit(solution)/shard_map/all_to_all | solution.py:107
  381.5 3.2 fusion.48
  384.7 3.2 fusion.51
  387.9 3.2 fusion.54
  391.1 3.3 fusion.57
  (75 shorter events, 44.3 us)
Async XLA Ops:
  6.5 1.7 copy-start
  6.5 1.9 copy-start.8
  6.5 18.7 %all-gather.3.cloned.1.call-start = ((), (), s32[]{:S(2)}) async-start(), calls=%async_computation.5 | async-start | bytes 7077888 | tf_op jit(solution)/shard_map/all_gather | solution.py:31
  7.3 294.2 %all-gather.5.cloned.1.call-start = ((), (), s32[]{:S(2)}) async-start(), calls=%async_computation.6 | async-start | bytes 37748736 | tf_op jit(solution)/shard_map/all_gather | solution.py:101
  9.3 1.5 collective-permute-start
  10.9 2.6 collective-permute-start.1
  13.5 2.6 collective-permute-start.2
  16.1 2.6 collective-permute-start.3
  18.7 3.5 collective-permute-start.4
  25.2 5.9 %copy-start.1 = (f32[384,3072]{1,0:T(8,128)S(1)}, f32[384,3072]{1,0:T(8,128)}, u32[]{:S(2)}) copy-start(f32[384,3072]{1,0:T(8,128)} %all-gather.3.cloned.1.call-done) | copy-start | bytes 14155780
  39.4 6.9 %copy-start.7 = (s32[8]{0:T(128)S(1)}, s32[8]{0:T(128)}, u32[]{:S(2)}) copy-start(s32[8]{0:T(128)} %param.7) | copy-start | bytes 100
  39.4 14.4 %slice-start = ((s8[4718592]{0:T(1024)(128)(4,1)}), s8[524288]{0:T(1024)(128)(4,1)S(1)}, s32[]{:S(2)}) async-start(s8[4718592]{0:T(1024)(128)(4,1)} %bitcast.127), calls=%async_computation.7 | async-start | bytes 1048576
  39.4 77.1 %all-to-all-start = ((f32[16,1,4,24,512]{4,3,2,1,0:T(8,128)}), f32[16,1,4,24,512]{4,3,2,1,0:T(8,128)}, u32[]{:S(2)}, u32[]{:S(2)}) async-start(f32[16,1,4,24,512]{4,3,2,1,0:T(8,128)} %maximum_bitcast_fusion.1), calls=%async_computation | async-start | bytes 6291456 | tf_op jit(solution)/shard_map/all_to_all | solution.py:129
  46.7 7.1 %slice-start.1 = ((s8[4718592]{0:T(1024)(128)(4,1)}), s8[4194304]{0:T(1024)(128)(4,1)S(1)}, s32[]{:S(2)}) async-start(s8[4718592]{0:T(1024)(128)(4,1)} %bitcast.127), calls=%async_computation.8 | async-start | bytes 8388608
  123.0 1.9 copy-start.2
  280.9 4.6 %copy-start.3 = (f32[16,1,4,24,512]{4,3,2,1,0:T(8,128)S(1)}, f32[16,1,4,24,512]{4,3,2,1,0:T(8,128)}, u32[]{:S(2)}) copy-start(f32[16,1,4,24,512]{4,3,2,1,0:T(8,128)} %get-tuple-element.14) | copy-start | bytes 9437188
  294.9 76.7 %all-to-all-start.3 = ((f32[16,1,4,24,512]{4,2,3,1,0:T(4,128)}), f32[16,1,4,24,512]{4,2,3,1,0:T(4,128)}, u32[]{:S(2)}, u32[]{:S(2)}) async-start(f32[16,1,4,24,512]{4,2,3,1,0:T(4,128)} %copy.79), calls=%async_computation.3 | async-start | bytes 6291456 | tf_op jit(solution)/shard_map/all_to_all | solution.py:129
  301.4 3.6 copy-start.4
  391.1 3.3 copy-start.5
  391.1 3.3 copy-start.6
Sparse Core Ops, SparseCore 0:
  8.9 16.2 all-gather.2
  26.8 41.4 all-gather.4

commit v6 on v5

--- a/solution.py
+++ b/solution.py
@@ -104,7 +104,18 @@
 
     def model_of(c, returned):
         picked = returned.transpose(1, 0, 2, 3).reshape(blocks, groups, own_rows, chunk)
-        picked = lax.all_to_all(picked, "mode", 1, 1, tiled=True)
+        if c == K_CHUNKS - 1:
+            picked = lax.all_to_all(picked, "mode", 1, 1, tiled=True)
+        else:
+            from_each = [lax.dynamic_index_in_dim(picked, mode_index, 1, keepdims=False)]
+            for shift in range(1, groups):
+                target = (mode_index + shift) % groups
+                sent = lax.dynamic_index_in_dim(picked, target, 1, keepdims=False)
+                pairs = [(m, (m + shift) % groups) for m in range(groups)]
+                from_each.append(lax.ppermute(sent, "mode", pairs))
+            stacked = jnp.stack(from_each, axis=1)
+            order = (mode_index - jnp.arange(groups, dtype=jnp.int32)) % groups
+            picked = jnp.take(stacked, order, axis=1)
         return jnp.concatenate(
             [
                 jnp.einsum(

time: 405 us -> 399 us (0.985)
  waiting for transfers between devices: 124 us -> 104 us
  blocking collectives: 157 us -> 149 us
  local copies, waits for them, and re-layouts: 17.8 us -> 25.5 us
  other arithmetic: 10 us -> 17.5 us
    all_to_all x2, waiting for transfers between devices: 112 us -> 90 us  [local(): lax.all_to_all(jnp.stack(sending, axis=1), 'pix', 0, 0, tiled=True)]
    all_to_all x2 -> x1, blocking collectives: 15.9 us -> 7.58 us  [model_of(): picked = lax.all_to_all(picked, 'mode', 1, 1, tiled=True)]
    gather x0 -> x1, local copies, waits for them, and re-layouts: none -> 4.37 us  [model_of(): picked = jnp.take(stacked, order, axis=1)]
    select_n x0 -> x2, other arithmetic: none -> 4.09 us  [model_of(): picked = jnp.take(stacked, order, axis=1)]
  transfers between devices with their start and end apart: 9 -> 10, of which waited for: 8 -> 9; matrix products, arithmetic and copies ran while one was open for 19% -> 23% of each run, Pallas kernels for 0% -> 0%
where the time goes in v6:
time: 399 us; the launch traced here: 393 us
  blocking collectives  149 us (37%)
  waiting for transfers between devices  104 us (26%)
  matrix products  64.4 us (16%)
  local copies, waits for them, and re-layouts  25.5 us (6%)
  starting transfers between devices  19.7 us (5%)
  other arithmetic  17.5 us (4%)
  between operations  14 us (4%)
    all_to_all x1, blocking collectives, local(): lax.all_to_all(jnp.stack(sending, axis=1), 'pix', 0, 0, tiled=True)  141 us
    all_to_all x2, waiting for transfers between devices, local(): lax.all_to_all(jnp.stack(sending, axis=1), 'pix', 0, 0, tiled=True)  90 us
    dot_general x8, matrix products, model_of(): jnp.einsum('mfk,mkp->fp', picked[b], whole_basis[:, c * chunk:(c + 1) * c...  26 us
    dot_general x8, matrix products, outbound(): jnp.dot(centered[b], pieces[c][b].T, precision=PRODUCT_PRECISION)  24.1 us
    dot_general x2, matrix products, inbound(): jnp.einsum('cb,bfk->cfk', same_annulus, arrived.reshape(parts * blocks, r...  12.7 us
    all_to_all x2, starting transfers between devices, local(): lax.all_to_all(jnp.stack(sending, axis=1), 'pix', 0, 0, tiled=True)  12.2 us
    another operation x3, local copies, waits for them, and re-layouts, local(): jnp.stack(sending, axis=1)  11.1 us
    ppermute x5, waiting for transfers between devices, butterfly_sum(): value = value + lax.ppermute(value, axes, pairs)  8.15 us
  transfers between devices with their start and end apart: 10, of which 9 were waited for; matrix products, arithmetic and copies ran while one was open for 23% of the time, Pallas kernels for 0%

profile of v6, /device:TPU:13, one launch (start us, length us, event | category | flops | bytes accessed | tf_op | source)
XLA Modules:
  0.0 393.2 jit_solution(11390340666886089882)
XLA Ops:
  25.2 3.0 fusion.27
  39.4 7.2 %all-to-all-start = ((f32[16,1,4,24,512]{4,3,2,1,0:T(8,128)}), f32[16,1,4,24,512]{4,3,2,1,0:T(8,128)}, u32[]{:S(2)}, u32[]{:S(2)}) async-start(f32[16,1,4,24,512]{4,3,2,1,0:T(8,128)} %maximum_bitcast_fusion.1), calls=%async_computation | async-start | bytes 6291456 | tf_op jit(solution)/shard_map/all_to_all | solution.py:140
  47.4 3.5 fusion.35
  50.9 3.6 fusion.33
  62.2 55.0 %all-to-all-done = f32[16,1,4,24,512]{4,3,2,1,0:T(8,128)} async-done(((f32[16,1,4,24,512]{4,3,2,1,0:T(8,128)}), f32[16,1,4,24,512]{4,3,2,1,0:T(8,128)}, u32[]{:S(2)}, u32[]{:S(2)}) %all-to-all-start) | async-done | bytes 3145760 | tf_op jit(solution)/shard_map/all_to_all | solution.py:140
  117.2 6.5 %broadcast_multiply_fusion.1 = f32[64,24,512]{2,0,1:T(8,128)S(1)} fusion(f32[64,512]{1,0:T(8,128)S(1)} %get-tuple-element.22, f32[64,64,1]{1,0,2:T(8,128)S(1)} %convolution_bitcast_fusion, f32[64,24,512]{2,1,0:T(8,128)} %bitcast.30), kind=kOutput, calls=%fused_computation.32 | convolution fusion | flops 604766208 | bytes 6438912 | tf_op jit(solution)/shard_map/cb,bfk->cfk/dot_general | solution.py:92
  126.8 141.0 %all_to_all.20 = f32[16,2,4,24,512]{4,3,2,1,0:T(8,128)S(1)} all-to-all(f32[16,2,4,24,512]{4,3,2,1,0:T(8,128)S(1)} %pad_maximum_fusion), channel_id=1, replica_groups=mesh['pix'=16,'mode'=2] {'pix'}, dimensions={0} | all-to-all | bytes 12582912 | tf_op jit(solution)/shard_map/all_to_all | solution.py:140
  270.3 6.2 %broadcast_multiply_fusion = f32[64,24,512]{2,0,1:T(8,128)} fusion(f32[64,512]{1,0:T(8,128)S(1)} %get-tuple-element.21, f32[64,64,1]{1,0,2:T(8,128)S(1)} %convolution_bitcast_fusion, f32[64,24,512]{2,1,0:T(8,128)S(1)} %bitcast.128), kind=kOutput, calls=%fused_computation.30 | convolution fusion | flops 604766208 | bytes 6438912 | tf_op jit(solution)/shard_map/cb,bfk->cfk/dot_general | solution.py:92
  276.5 4.8 %stack_reshape.7 = f32[16,1,4,24,512]{4,2,0,3,1:T(4,128)} reshape(f32[64,24,512]{2,0,1:T(8,128)} %broadcast_multiply_fusion) | data formatting | bytes 6291456 | tf_op jit(solution)/shard_map/stack;reshape | solution.py:140
  281.3 4.5 %copy.50 = f32[16,1,4,24,512]{4,2,3,1,0:T(4,128)} copy(f32[16,1,4,24,512]{4,2,0,3,1:T(4,128)} %stack_reshape.7) | data formatting | bytes 6291456 | tf_op jit(solution)/shard_map/stack;reshape | solution.py:140
  285.8 5.0 %all-to-all-start.2 = ((f32[16,1,4,24,512]{4,2,3,1,0:T(4,128)}), f32[16,1,4,24,512]{4,2,3,1,0:T(4,128)}, u32[]{:S(2)}, u32[]{:S(2)}) async-start(f32[16,1,4,24,512]{4,2,3,1,0:T(4,128)} %copy.50), calls=%async_computation.2 | async-start | bytes 6291456 | tf_op jit(solution)/shard_map/all_to_all | solution.py:140
  301.2 3.3 pad_maximum_fusion.1
  304.5 4.4 %gather_fusion = f32[2,4,192,512]{3,2,1,0:T(8,128)} fusion(f32[4,2,192,512]{3,2,1,0:T(8,128)} %pad_maximum_fusion.1, s32[1024]{0:T(1024)S(1)} %pad_clamp_fusion), kind=kCustom, calls=%fused_computation | custom fusion | bytes 6291464 | tf_op jit(solution)/shard_map/jit(_take)/gather | solution.py:118
  308.9 4.1 %fusion.20 = f32[4,2,192,512]{3,2,1,0:T(8,128)} fusion(f32[2,4,192,512]{3,2,1,0:T(8,128)} %gather_fusion, pred[2]{0:T(512)(128)(4,1)S(1)} %compare_and_fusion), kind=kLoop, calls=%fused_computation.27 | loop fusion | flops 786432 | bytes 6291458 | tf_op jit(solution)/shard_map/jit(_take)/select_n | solution.py:118
  313.0 3.5 fusion.37
  316.6 3.2 fusion.40
  319.7 3.2 fusion.43
  322.9 3.2 fusion.46
  326.1 35.0 %all-to-all-done.2 = f32[16,1,4,24,512]{4,2,3,1,0:T(4,128)} async-done(((f32[16,1,4,24,512]{4,2,3,1,0:T(4,128)}), f32[16,1,4,24,512]{4,2,3,1,0:T(4,128)}, u32[]{:S(2)}, u32[]{:S(2)}) %all-to-all-start.2) | async-done | bytes 3145760 | tf_op jit(solution)/shard_map/all_to_all | solution.py:140
  363.9 7.6 %all_to_all.21 = f32[4,2,192,512]{3,2,0,1:T(8,128)S(1)} all-to-all(f32[4,2,192,512]{3,2,0,1:T(8,128)S(1)} %copy.51), channel_id=1, replica_groups=mesh['pix'=16,'mode'=2] {'mode'}, dimensions={1} | all-to-all | bytes 6291456 | tf_op jit(solution)/shard_map/all_to_all | solution.py:108
  371.5 3.2 fusion.49
  374.7 3.2 fusion.52
  377.9 3.2 fusion.55
  381.1 3.3 fusion.58
  (82 shorter events, 58.5 us)
Async XLA Ops:
  6.5 1.7 copy-start
  6.5 1.9 copy-start.8
  6.5 18.7 %all-gather.3.cloned.1.call-start = ((), (), s32[]{:S(2)}) async-start(), calls=%async_computation.4 | async-start | bytes 7077888 | tf_op jit(solution)/shard_map/all_gather | solution.py:31
  7.3 305.7 %all-gather.5.cloned.1.call-start = ((), (), s32[]{:S(2)}) async-start(), calls=%async_computation.5 | async-start | bytes 37748736 | tf_op jit(solution)/shard_map/all_gather | solution.py:101
  9.3 1.5 collective-permute-start
  10.9 2.6 collective-permute-start.1
  13.5 2.6 collective-permute-start.2
  16.1 2.6 collective-permute-start.3
  18.7 3.5 collective-permute-start.4
  25.2 5.9 %copy-start.1 = (f32[384,3072]{1,0:T(8,128)S(1)}, f32[384,3072]{1,0:T(8,128)}, u32[]{:S(2)}) copy-start(f32[384,3072]{1,0:T(8,128)} %all-gather.3.cloned.1.call-done) | copy-start | bytes 14155780
  39.4 7.6 %copy-start.7 = (s32[8]{0:T(128)S(1)}, s32[8]{0:T(128)}, u32[]{:S(2)}) copy-start(s32[8]{0:T(128)} %param.7) | copy-start | bytes 100
  39.4 15.2 %slice-start = ((s8[4718592]{0:T(1024)(128)(4,1)}), s8[524288]{0:T(1024)(128)(4,1)S(1)}, s32[]{:S(2)}) async-start(s8[4718592]{0:T(1024)(128)(4,1)} %bitcast.126), calls=%async_computation.6 | async-start | bytes 1048576
  39.4 77.8 %all-to-all-start = ((f32[16,1,4,24,512]{4,3,2,1,0:T(8,128)}), f32[16,1,4,24,512]{4,3,2,1,0:T(8,128)}, u32[]{:S(2)}, u32[]{:S(2)}) async-start(f32[16,1,4,24,512]{4,3,2,1,0:T(8,128)} %maximum_bitcast_fusion.1), calls=%async_computation | async-start | bytes 6291456 | tf_op jit(solution)/shard_map/all_to_all | solution.py:140
  47.3 7.2 %slice-start.1 = ((s8[4718592]{0:T(1024)(128)(4,1)}), s8[4194304]{0:T(1024)(128)(4,1)S(1)}, s32[]{:S(2)}) async-start(s8[4718592]{0:T(1024)(128)(4,1)} %bitcast.126), calls=%async_computation.7 | async-start | bytes 8388608
  123.7 1.9 copy-start.2
  285.8 75.3 %all-to-all-start.2 = ((f32[16,1,4,24,512]{4,2,3,1,0:T(4,128)}), f32[16,1,4,24,512]{4,2,3,1,0:T(4,128)}, u32[]{:S(2)}, u32[]{:S(2)}) async-start(f32[16,1,4,24,512]{4,2,3,1,0:T(4,128)} %copy.50), calls=%async_computation.2 | async-start | bytes 6291456 | tf_op jit(solution)/shard_map/all_to_all | solution.py:140
  295.0 6.2 %collective-permute-start.5 = (f32[4,192,512]{2,1,0:T(8,128)}, f32[4,192,512]{2,1,0:T(8,128)}, u32[]{:S(2)}, u32[]{:S(2)}) collective-permute-start(f32[4,192,512]{2,1,0:T(8,128)} %get-tuple-element.16), channel_id=1, source_target_pairs={{0,1},{1,0},{2,3},{3,2},{4,5},{5,4},{6,7},{7,6},{8,9},{9,8},{10,11... | collective-permute-start | bytes 4718600 | tf_op jit(solution)/shard_map/ppermute | solution.py:115
  297.8 3.4 copy-start.4
  313.0 3.6 copy-start.3
  381.1 3.3 copy-start.5
  381.1 3.3 copy-start.6
Sparse Core Ops, SparseCore 0:
  8.9 16.2 all-gather.2
  26.8 41.4 all-gather.4

commit v7 on v2

--- a/solution.py
+++ b/solution.py
@@ -62,29 +62,23 @@
     retained = (mode_ids[None, :] < truncation[:, None]).astype(jnp.float32)
     annulus_means = annulus_totals / pixel_counts[:, None]
     block_means = jnp.einsum("ba,af->bf", onehot, annulus_means, precision=HIGHEST_PRECISION)
-    centered = [
-        gathered[:, b * block_len : (b + 1) * block_len] - block_means[b][:, None]
-        for b in range(blocks)
-    ]
     chunk = modes_dev // K_CHUNKS
     same_annulus = jnp.einsum("ca,ba->cb", every_onehot, every_onehot, precision=HIGHEST_PRECISION)
     block_retained = jnp.einsum("ba,ak->bk", every_onehot, retained, precision=HIGHEST_PRECISION)
     rows_dev = total_frames // parts
-    pieces = [
-        [
-            basis[c * chunk : (c + 1) * chunk, b * block_len : (b + 1) * block_len]
-            for b in range(blocks)
-        ]
-        for c in range(K_CHUNKS)
-    ]
+
+    def piece_of(c, b):
+        return lax.dynamic_slice(basis, (c * chunk, b * block_len), (chunk, block_len))
 
     def outbound(c):
-        per_block = jnp.stack(
-            [
-                jnp.dot(centered[b], pieces[c][b].T, precision=PRODUCT_PRECISION)
-                for b in range(blocks)
-            ],
-            axis=0,
+        def body(b, per_block):
+            mean = lax.dynamic_index_in_dim(block_means, b, 0, keepdims=False)
+            centered = lax.dynamic_slice_in_dim(gathered, b * block_len, block_len, 1) - mean[:, None]
+            product = jnp.dot(centered, piece_of(c, b).T, precision=PRODUCT_PRECISION)
+            return lax.dynamic_update_index_in_dim(per_block, product, b, 0)
+
+        per_block = lax.fori_loop(
+            0, blocks, body, jnp.zeros((blocks, total_frames, chunk), jnp.float32)
         )
         return per_block.reshape(blocks, parts, rows_dev, chunk).transpose(1, 0, 2, 3)
 
@@ -100,10 +94,13 @@
 
     def model_of(c, returned):
         picked = returned.transpose(1, 0, 2, 3).reshape(blocks, total_frames, chunk)
-        return jnp.concatenate(
-            [jnp.dot(picked[b], pieces[c][b], precision=PRODUCT_PRECISION) for b in range(blocks)],
-            axis=1,
-        )
+
+        def body(b, term):
+            coefficients = lax.dynamic_index_in_dim(picked, b, 0, keepdims=False)
+            product = jnp.dot(coefficients, piece_of(c, b), precision=PRODUCT_PRECISION)
+            return lax.dynamic_update_slice_in_dim(term, product, b * block_len, 1)
+
+        return lax.fori_loop(0, blocks, body, jnp.zeros((total_frames, pix_dev), jnp.float32))
 
     term = None
     pending = None

time: 393 us -> 528 us (1.34)
  local copies, waits for them, and re-layouts: 13.2 us -> 199 us
  waiting for transfers between devices: 135 us -> 66.1 us
  matrix products: 59 us -> 66.8 us
    dynamic_update_slice x0 -> x16, local copies, waits for them, and re-layouts: none -> 134 us  [body(): return lax.dynamic_update_index_in_dim(per_block, product, b, 0)]
    all_to_all x2, waiting for transfers between devices: 111 us -> 42.7 us  [local(): lax.all_to_all(jnp.stack(sending, axis=1), 'pix', 0, 0, tiled=True)]
    dynamic_slice x0 -> x16, local copies, waits for them, and re-layouts: none -> 20.7 us  [the longest x8 20.5 us: body(): coefficients = lax.dynamic_index_in_dim(picked, b, 0, keepdims=False)]
    another operation x0 -> x6, local copies, waits for them, and re-layouts: none -> 19.7 us  [the longest x2 9.87 us: inbound(): arrived.reshape(parts * blocks, rows_dev, chunk)]
    another operation x2 -> x3, local copies, waits for them, and re-layouts: 5.33 us -> 14.1 us  [local(): jnp.stack(sending, axis=1)]
    dot_general x16, matrix products: 46.1 us -> 52.4 us  [the longest x8 29.3 us: body(): product = jnp.dot(coefficients, piece_of(c, b), precision=PRODUCT_PRECISION)]
  transfers between devices with their start and end apart: 9 -> 9, of which waited for: 9 -> 8; matrix products, arithmetic and copies ran while one was open for 8% -> 22% of each run, Pallas kernels for 0% -> 0%
where the time goes in v7:
time: 528 us; the launch traced here: 522 us
  local copies, waits for them, and re-layouts  199 us (38%)
  blocking collectives  143 us (27%)
  matrix products  66.8 us (13%)
  waiting for transfers between devices  66.1 us (13%)
  other arithmetic  17.6 us (3%)
  starting transfers between devices  16 us (3%)
  between operations  13.5 us (3%)
    all_to_all x1, blocking collectives, local(): lax.all_to_all(jnp.stack(sending, axis=1), 'pix', 0, 0, tiled=True)  143 us
    dynamic_update_slice x16, local copies, waits for them, and re-layouts, body(): return lax.dynamic_update_index_in_dim(per_block, product, b, 0)  134 us
    all_to_all x2, waiting for transfers between devices, local(): lax.all_to_all(jnp.stack(sending, axis=1), 'pix', 0, 0, tiled=True)  42.7 us
    dot_general x8, matrix products, body(): product = jnp.dot(coefficients, piece_of(c, b), precision=PRODUCT_PRECISION)  29.3 us
    dot_general x8, matrix products, body(): product = jnp.dot(centered, piece_of(c, b).T, precision=PRODUCT_PRECISION)  23.1 us
    dynamic_slice x8, local copies, waits for them, and re-layouts, body(): coefficients = lax.dynamic_index_in_dim(picked, b, 0, keepdims=False)  20.5 us
    another operation x3, local copies, waits for them, and re-layouts, local(): jnp.stack(sending, axis=1)  14.1 us
    dot_general x2, matrix products, inbound(): jnp.einsum('cb,bfk->cfk', same_annulus, arrived.reshape(parts * blocks, r...  12.7 us
  transfers between devices with their start and end apart: 9, of which 8 were waited for; matrix products, arithmetic and copies ran while one was open for 22% of the time, Pallas kernels for 0%

profile of v7, /device:TPU:13, one launch (start us, length us, event | category | flops | bytes accessed | tf_op | source)
XLA Modules:
  0.0 522.3 jit_solution(12102426613418549742)
XLA Ops:
  27.4 78.8 %while.53 = (s32[]{:T(128)}, f32[4,384,512]{2,0,1:T(4,128)}, f32[384,3072]{1,0:T(8,128)}, f32[4,384]{1,0:T(4,128)S(1)}, f32[1024,3072]{1,0:T(8,128)}, /*index=5*/s32[]{:T(128)}, s32[]{:T(128)}, s32[]{:T(128)}, s32[]{:T(128)}) while((s32[]{:T(128)}, f32[4,384,512]{2,0,1:T(4,128)}, f32[384,3072]{1,0:T(8,128)}, f32[4,384]{1,0:T(4,128)S(1)}, ...), condition=%wide.region_8.9_spmd, body=%wide.region_7.8_spmd.sunk | while | flops 906264576 | bytes 6690451 | solution.py:80
  31.1 16.0 %dynamic_update_slice.36 = f32[4,384,512]{2,0,1:T(4,128)} dynamic-update-slice(f32[4,384,512]{2,0,1:T(4,128)} %get-tuple-element.572, f32[1,384,512]{2,0,1:T(1,128)S(1)} %copy.56, s32[]{:T(128)} %get-tuple-element.571, s32[]{:T(128)} %constant.181.clone.1..sunk.1, s32[]{:T(128)} %constant.181.clone.1..sunk.1) | dynamic-update-slice | bytes 1572868 | tf_op jit(solution)/shard_map/while/body/eval_jaxpr/jit(dynamic_update_index_in_dim)/dynamic_update_slice | solution.py:78
  50.8 16.0 %dynamic_update_slice.36 = f32[4,384,512]{2,0,1:T(4,128)} dynamic-update-slice(f32[4,384,512]{2,0,1:T(4,128)} %get-tuple-element.572, f32[1,384,512]{2,0,1:T(1,128)S(1)} %copy.56, s32[]{:T(128)} %get-tuple-element.571, s32[]{:T(128)} %constant.181.clone.1..sunk.1, s32[]{:T(128)} %constant.181.clone.1..sunk.1) | dynamic-update-slice | bytes 1572868 | tf_op jit(solution)/shard_map/while/body/eval_jaxpr/jit(dynamic_update_index_in_dim)/dynamic_update_slice | solution.py:78
  70.5 16.0 %dynamic_update_slice.36 = f32[4,384,512]{2,0,1:T(4,128)} dynamic-update-slice(f32[4,384,512]{2,0,1:T(4,128)} %get-tuple-element.572, f32[1,384,512]{2,0,1:T(1,128)S(1)} %copy.56, s32[]{:T(128)} %get-tuple-element.571, s32[]{:T(128)} %constant.181.clone.1..sunk.1, s32[]{:T(128)} %constant.181.clone.1..sunk.1) | dynamic-update-slice | bytes 1572868 | tf_op jit(solution)/shard_map/while/body/eval_jaxpr/jit(dynamic_update_index_in_dim)/dynamic_update_slice | solution.py:78
  90.2 16.0 %dynamic_update_slice.36 = f32[4,384,512]{2,0,1:T(4,128)} dynamic-update-slice(f32[4,384,512]{2,0,1:T(4,128)} %get-tuple-element.572, f32[1,384,512]{2,0,1:T(1,128)S(1)} %copy.56, s32[]{:T(128)} %get-tuple-element.571, s32[]{:T(128)} %constant.181.clone.1..sunk.1, s32[]{:T(128)} %constant.181.clone.1..sunk.1) | dynamic-update-slice | bytes 1572868 | tf_op jit(solution)/shard_map/while/body/eval_jaxpr/jit(dynamic_update_index_in_dim)/dynamic_update_slice | solution.py:78
  106.2 6.5 %all-to-all-start = ((f32[16,1,4,24,512]{4,2,3,1,0:T(4,128)}), f32[16,1,4,24,512]{4,2,3,1,0:T(4,128)}, u32[]{:S(2)}, u32[]{:S(2)}) async-start(f32[16,1,4,24,512]{4,2,3,1,0:T(4,128)} %bitcast.64), calls=%async_computation | async-start | bytes 6291456 | tf_op jit(solution)/shard_map/all_to_all | solution.py:113
  115.7 78.9 %while.52 = (s32[]{:T(128)}, f32[4,384,512]{2,0,1:T(4,128)}, f32[384,3072]{1,0:T(8,128)}, f32[4,384]{1,0:T(4,128)S(1)}, f32[1024,3072]{1,0:T(8,128)}, /*index=5*/s32[]{:T(128)}, s32[]{:T(128)}, s32[]{:T(128)}, s32[]{:T(128)}) while((s32[]{:T(128)}, f32[4,384,512]{2,0,1:T(4,128)}, f32[384,3072]{1,0:T(8,128)}, f32[4,384]{1,0:T(4,128)S(1)}, ...), condition=%wide.region_6.7_spmd, body=%wide.region_5.6_spmd.sunk | while | flops 906264576 | bytes 6690451 | solution.py:80
  119.4 16.0 %dynamic_update_slice.35 = f32[4,384,512]{2,0,1:T(4,128)} dynamic-update-slice(f32[4,384,512]{2,0,1:T(4,128)} %get-tuple-element.545, f32[1,384,512]{2,0,1:T(1,128)S(1)} %copy.55, s32[]{:T(128)} %get-tuple-element.544, s32[]{:T(128)} %constant.181.clone.1..sunk, s32[]{:T(128)} %constant.181.clone.1..sunk) | dynamic-update-slice | bytes 1572868 | tf_op jit(solution)/shard_map/while/body/eval_jaxpr/jit(dynamic_update_index_in_dim)/dynamic_update_slice | solution.py:78
  139.1 16.0 %dynamic_update_slice.35 = f32[4,384,512]{2,0,1:T(4,128)} dynamic-update-slice(f32[4,384,512]{2,0,1:T(4,128)} %get-tuple-element.545, f32[1,384,512]{2,0,1:T(1,128)S(1)} %copy.55, s32[]{:T(128)} %get-tuple-element.544, s32[]{:T(128)} %constant.181.clone.1..sunk, s32[]{:T(128)} %constant.181.clone.1..sunk) | dynamic-update-slice | bytes 1572868 | tf_op jit(solution)/shard_map/while/body/eval_jaxpr/jit(dynamic_update_index_in_dim)/dynamic_update_slice | solution.py:78
  158.8 16.0 %dynamic_update_slice.35 = f32[4,384,512]{2,0,1:T(4,128)} dynamic-update-slice(f32[4,384,512]{2,0,1:T(4,128)} %get-tuple-element.545, f32[1,384,512]{2,0,1:T(1,128)S(1)} %copy.55, s32[]{:T(128)} %get-tuple-element.544, s32[]{:T(128)} %constant.181.clone.1..sunk, s32[]{:T(128)} %constant.181.clone.1..sunk) | dynamic-update-slice | bytes 1572868 | tf_op jit(solution)/shard_map/while/body/eval_jaxpr/jit(dynamic_update_index_in_dim)/dynamic_update_slice | solution.py:78
  178.5 16.0 %dynamic_update_slice.35 = f32[4,384,512]{2,0,1:T(4,128)} dynamic-update-slice(f32[4,384,512]{2,0,1:T(4,128)} %get-tuple-element.545, f32[1,384,512]{2,0,1:T(1,128)S(1)} %copy.55, s32[]{:T(128)} %get-tuple-element.544, s32[]{:T(128)} %constant.181.clone.1..sunk, s32[]{:T(128)} %constant.181.clone.1..sunk) | dynamic-update-slice | bytes 1572868 | tf_op jit(solution)/shard_map/while/body/eval_jaxpr/jit(dynamic_update_index_in_dim)/dynamic_update_slice | solution.py:78
  199.0 4.9 reshape_squeeze.6
  203.9 6.3 %broadcast_multiply_fusion.1 = f32[64,24,512]{2,0,1:T(8,128)} fusion(f32[64,512]{1,0:T(8,128)S(1)} %get-tuple-element.418, f32[64,64,1]{1,0,2:T(8,128)S(1)} %convolution_bitcast_fusion, f32[64,24,512]{2,0,1:T(8,128)} %reshape_squeeze.6), kind=kOutput, calls=%fused_computation.32 | convolution fusion | flops 604766208 | bytes 6438912 | tf_op jit(solution)/shard_map/cb,bfk->cfk/dot_general | solution.py:86
  210.3 4.8 stack_reshape.6
  219.7 142.7 %all_to_all.15 = f32[16,2,4,24,512]{4,2,3,1,0:T(4,128)S(1)} all-to-all(f32[16,2,4,24,512]{4,2,3,1,0:T(4,128)S(1)} %pad_maximum_fusion), channel_id=1, replica_groups=mesh['pix'=16,'mode'=2] {'pix'}, dimensions={0} | all-to-all | bytes 12582912 | tf_op jit(solution)/shard_map/all_to_all | solution.py:113
  368.2 4.9 reshape_squeeze.7
  373.1 6.4 %broadcast_multiply_fusion = f32[64,24,512]{2,0,1:T(8,128)} fusion(f32[64,512]{1,0:T(8,128)S(1)} %get-tuple-element.417, f32[64,64,1]{1,0,2:T(8,128)S(1)} %convolution_bitcast_fusion, f32[64,24,512]{2,0,1:T(8,128)} %reshape_squeeze.7), kind=kOutput, calls=%fused_computation.31 | convolution fusion | flops 604766208 | bytes 6438912 | tf_op jit(solution)/shard_map/cb,bfk->cfk/dot_general | solution.py:86
  379.5 4.8 stack_reshape.7
  388.7 4.8 all-to-all-start.2
  396.4 24.9 %while.54 = (s32[]{:T(128)}, f32[384,3072]{1,0:T(8,128)}, f32[4,384,512]{2,0,1:T(4,128)}, f32[1024,3072]{1,0:T(8,128)}, s32[]{:T(128)}, /*index=5*/s32[]{:T(128)}, s32[]{:T(128)}, s32[]{:T(128)}) while((s32[]{:T(128)}, f32[384,3072]{1,0:T(8,128)}, f32[4,384,512]{2,0,1:T(4,128)}, f32[1024,3072]{1,0:T(8,128)}, s32[]{:T(128)}, ...), condition=%wide.region_10.11_spmd, body=%wide.region_9.10_spmd.sunk | while | flops 905969664 | bytes 5112967 | solution.py:103
  421.4 42.7 %all-to-all-done.2 = f32[16,1,4,24,512]{4,2,3,1,0:T(4,128)} async-done(((f32[16,1,4,24,512]{4,2,3,1,0:T(4,128)}), f32[16,1,4,24,512]{4,2,3,1,0:T(4,128)}, u32[]{:S(2)}, u32[]{:S(2)}) %all-to-all-start.2) | async-done | bytes 3145760 | tf_op jit(solution)/shard_map/all_to_all | solution.py:113
  466.8 24.9 %while.55 = (s32[]{:T(128)}, f32[384,3072]{1,0:T(8,128)}, f32[4,384,512]{2,0,1:T(4,128)}, f32[1024,3072]{1,0:T(8,128)}, s32[]{:T(128)}, /*index=5*/s32[]{:T(128)}, s32[]{:T(128)}, s32[]{:T(128)}) while((s32[]{:T(128)}, f32[384,3072]{1,0:T(8,128)}, f32[4,384,512]{2,0,1:T(4,128)}, f32[1024,3072]{1,0:T(8,128)}, s32[]{:T(128)}, ...), condition=%wide.region_12.13_spmd, body=%wide.region_11.12_spmd.sunk | while | flops 905969664 | bytes 5112967 | solution.py:103
  491.7 6.9 %add.186 = f32[384,3072]{1,0:T(8,128)} add(f32[384,3072]{1,0:T(8,128)} %get-tuple-element.353, f32[384,3072]{1,0:T(8,128)} %get-tuple-element.354) | non-fusion elementwise | flops 1179648 | bytes 14155776 | tf_op jit(solution)/shard_map/add | solution.py:121
  499.9 11.8 %reduce-scatter.2.cloned.1.call-done = f32[192,3072]{1,0:T(8,128)} async-done(((f32[384,3072]{1,0:T(8,128)}), f32[192,3072]{1,0:T(8,128)}) %reduce-scatter.2.cloned.1.call-update) | async-done | bytes 2359312 | tf_op jit(solution)/shard_map/reduce_scatter | solution.py:123
  (95 shorter events, 133.1 us)
Async XLA Ops:
  6.5 1.7 copy-start
  6.5 1.9 copy-start.2
  6.5 18.7 %all-gather.2.cloned.1.call-start = ((), (), s32[]{:S(2)}) async-start(), calls=%async_computation.4 | async-start | bytes 7077888 | tf_op jit(solution)/shard_map/all_gather | solution.py:31
  9.3 1.5 collective-permute-start
  10.9 2.6 collective-permute-start.1
  13.5 2.6 collective-permute-start.2
  16.1 2.6 collective-permute-start.3
  18.7 3.5 collective-permute-start.4
  106.2 6.9 %copy-start.1 = (s32[8]{0:T(128)S(1)}, s32[8]{0:T(128)}, u32[]{:S(2)}) copy-start(s32[8]{0:T(128)} %param.15) | copy-start | bytes 100
  106.2 88.3 %all-to-all-start = ((f32[16,1,4,24,512]{4,2,3,1,0:T(4,128)}), f32[16,1,4,24,512]{4,2,3,1,0:T(4,128)}, u32[]{:S(2)}, u32[]{:S(2)}) async-start(f32[16,1,4,24,512]{4,2,3,1,0:T(4,128)} %bitcast.64), calls=%async_computation | async-start | bytes 6291456 | tf_op jit(solution)/shard_map/all_to_all | solution.py:113
  388.7 75.3 %all-to-all-start.2 = ((f32[16,1,4,24,512]{4,2,3,1,0:T(4,128)}), f32[16,1,4,24,512]{4,2,3,1,0:T(4,128)}, u32[]{:S(2)}, u32[]{:S(2)}) async-start(f32[16,1,4,24,512]{4,2,3,1,0:T(4,128)} %copy.31), calls=%async_computation.2 | async-start | bytes 6291456 | tf_op jit(solution)/shard_map/all_to_all | solution.py:113
  393.6 118.2 %reduce-scatter.2.cloned.1.call-start = ((), (), s32[]{:S(2)}) async-start(), calls=%async_computation.5 | async-start | bytes 7077888 | tf_op jit(solution)/shard_map/reduce_scatter | solution.py:123
Sparse Core Ops, SparseCore 0:
  8.9 16.2 all-gather.1
  498.8 12.9 reduce-scatter.1
